TPU v7x, 256 devices: a whole 4x4x8 slice. The times are simulated.
256 devices in a mesh: patch: 8 (over z), tm: 8 (over y, core), subject: 4 (over x).
Axes of the slice: x: 4, y: 4, z: 8, core: 2. Of those that a mesh axis runs over, the one named last changes fastest.
Arguments:
- frames_in: bfloat16 [256, 512, 512], P(('subject', 'patch', 'tm')), parts along dimension 0, may hold values from -6 to 6
- spatial_qkv: bfloat16 [512, 1536], replicated, may hold values from -20 to 20, as said below
- spatial_out: bfloat16 [512, 512], replicated, may hold values from -0.25 to 0.25
- temporal_qkv: bfloat16 [512, 1536], replicated, may hold values from -20 to 20, as said below
- temporal_out: bfloat16 [512, 512], replicated, may hold values from -0.25 to 0.25
Outputs:
- frames_out: bfloat16 [256, 512, 512], P(('subject', 'patch', 'tm')), parts along dimension 0
There are 4 independent parts, one for each index of `subject`. A program takes and returns all parts, laid end to end along the dimension named above; an argument that names none is the same for every part. Nothing has to cross between parts.
Inputs may be any that keep to these rules, and one draw needn't show every extreme that they name: `spatial_qkv`: columns hold query, key and value projections in that order, each 8 heads of 64. `temporal_qkv`: columns hold query, key and value projections in that order, each 8 heads of 64.
All inputs are finite; a program needn't handle non-finite values.
Results may differ from a plain program's by a relative error of at most 0.015.
Values may be sent and summed in bfloat16 or wider, within the bound.
No kernel may reach another device: no remote copies, remote signals or barrier semaphores. Data moves between devices by JAX's collectives and lax.ppermute only.
A program may use at most 64 MiB of HBM per device.

v0:
```python
import jax
import jax.numpy as jnp
from jax import lax
from jax.sharding import PartitionSpec as P

HEADS = 8


epsilon = 1e-05
floor_score = -1e30


def layer_norm(input_rows):
    as_float = input_rows.astype(jnp.float32)
    centre = jnp.mean(as_float, axis=-1, keepdims=True)
    centered = as_float - centre
    spread = jnp.mean(centered * centered, axis=-1, keepdims=True)
    return (centered * lax.rsqrt(spread + epsilon)).astype(jnp.bfloat16)


def project_heads(input_rows, qkv_weight):
    model_width = input_rows.shape[-1]
    normed = layer_norm(input_rows)
    packed = jnp.dot(
        normed.reshape(-1, model_width), qkv_weight, preferred_element_type=jnp.float32
    ).astype(jnp.bfloat16)
    shaped = packed.reshape(input_rows.shape[:-1] + (3, HEADS, model_width // HEADS))
    return (shaped[..., 0, :, :], shaped[..., 1, :, :], shaped[..., 2, :, :])


def spatial_frame(one_frame, qkv_weight, out_weight):
    queries, key_rows, value_rows = project_heads(one_frame, qkv_weight)
    factor = queries.shape[-1] ** (-0.5)
    scores = (
        jnp.einsum("qhd,khd->hqk", queries, key_rows, preferred_element_type=jnp.float32) * factor
    )
    highest = jnp.max(scores, axis=-1, keepdims=True)
    exp_terms = jnp.exp(scores - highest)
    row_total = jnp.sum(exp_terms, axis=-1)
    mixture = jnp.einsum(
        "hqk,khd->qhd",
        exp_terms.astype(jnp.bfloat16),
        value_rows,
        preferred_element_type=jnp.float32,
    )
    mixture = (mixture / jnp.transpose(row_total)[:, :, None]).astype(jnp.bfloat16)
    update = jnp.dot(
        mixture.reshape(one_frame.shape), out_weight, preferred_element_type=jnp.float32
    )
    return (one_frame.astype(jnp.float32) + update).astype(jnp.bfloat16)


def causal_columns(columns, qkv_weight, out_weight):
    queries, key_rows, value_rows = project_heads(columns, qkv_weight)
    factor = queries.shape[-1] ** (-0.5)
    scores = (
        jnp.einsum("qchd,kchd->chqk", queries, key_rows, preferred_element_type=jnp.float32)
        * factor
    )
    frame_order = jnp.arange(columns.shape[0], dtype=jnp.int32)
    allowed = frame_order[None, :] <= frame_order[:, None]
    masked = jnp.where(allowed, scores, floor_score)
    highest = jnp.max(masked, axis=-1, keepdims=True)
    exp_terms = jnp.where(allowed, jnp.exp(masked - highest), 0.0)
    row_total = jnp.sum(exp_terms, axis=-1)
    mixture = jnp.einsum(
        "chqk,kchd->qchd",
        exp_terms.astype(jnp.bfloat16),
        value_rows,
        preferred_element_type=jnp.float32,
    )
    mixture = (mixture / jnp.transpose(row_total, (2, 0, 1))[..., None]).astype(jnp.bfloat16)
    model_width = columns.shape[-1]
    update = jnp.dot(
        mixture.reshape(-1, model_width), out_weight, preferred_element_type=jnp.float32
    )
    return (columns.astype(jnp.float32) + update.reshape(columns.shape)).astype(jnp.bfloat16)


def temporal_layer(columns, qkv_weight, out_weight):
    frame_total, column_count, model_width = columns.shape
    group_size = min(8, column_count)
    grouped = columns.reshape(
        frame_total, column_count // group_size, group_size, model_width
    ).transpose(1, 0, 2, 3)

    def group_step(group_cols):
        return causal_columns(group_cols, qkv_weight, out_weight)

    result = lax.map(group_step, grouped)
    return result.transpose(1, 0, 2, 3).reshape(frame_total, column_count, model_width)


def body(frames_in, spatial_qkv, spatial_out, temporal_qkv, temporal_out):

    def frame_step(one_frame):
        return spatial_frame(one_frame, spatial_qkv, spatial_out)

    hidden = lax.map(frame_step, frames_in)
    columns = lax.all_to_all(hidden, ("patch", "tm"), split_axis=1, concat_axis=0, tiled=True)
    result = temporal_layer(columns, temporal_qkv, temporal_out)
    return lax.all_to_all(result, ("patch", "tm"), split_axis=0, concat_axis=1, tiled=True)


def solution(mesh):
    in_specs = (P(("subject", "patch", "tm"), None, None), P(), P(), P(), P())
    out_specs = P(("subject", "patch", "tm"), None, None)
    return jax.shard_map(body, mesh=mesh, in_specs=in_specs, out_specs=out_specs, check_vma=False)
```

profile of v0, /device:TPU:1, one launch (start us, length us, event | category | flops | bytes accessed | tf_op | source)
XLA Modules:
  0.0 105.3 jit_solution(2717038934075363508)
XLA Ops:
  0.0 0.0 copy-start
  0.0 1.3 %convert_reduce_fusion = f32[512]{0:T(512)S(1)} fusion(bf16[1,512,512]{2,1,0:T(8,128)(2,1)} %param.5), kind=kLoop, calls=%fused_computation.18 | loop fusion | flops 523776 | bytes 526336 | tf_op jit(solution)/shard_map/while/body/eval_jaxpr/reduce_sum | solution.py:15
  1.3 1.3 %fusion.18 = f32[512]{0:T(512)S(1)} fusion(bf16[1,512,512]{2,1,0:T(8,128)(2,1)} %param.5, f32[512]{0:T(512)S(1)} %broadcast_multiply_fusion.1), kind=kLoop, calls=%fused_computation.26 | loop fusion | flops 1048064 | bytes 528384 | tf_op jit(solution)/shard_map/while/body/eval_jaxpr/reduce_sum | solution.py:17
  2.7 0.0 copy-done
  2.7 3.2 %convolution_convert_fusion.1 = bf16[512,1536]{1,0:T(8,128)(2,1)} fusion(bf16[512,1536]{1,0:T(8,128)(2,1)S(1)} %copy-done, bf16[1,512,512]{2,1,0:T(8,128)(2,1)} %param.5, f32[512]{0:T(512)S(1)} %add_rsqrt_fusion.1, f32[512]{0:T(512)S(1)} %broadcast_multiply_fusion.1), kind=kOutput, calls=%fused_computation.9 | convolution fusion | flops 807141376 | bytes 3674112 | tf_op jit(solution)/shard_map/while/body/eval_jaxpr/dot_general | solution.py:24
  5.9 1.7 %copy.22 = bf16[512,1536]{0,1:T(8,128)(2,1)S(1)} copy(bf16[512,1536]{1,0:T(8,128)(2,1)} %convolution_convert_fusion.1) | data formatting | bytes 3145728 | tf_op jit(solution)/shard_map/while/body/eval_jaxpr/convert_element_type | solution.py:26
  7.6 1.3 %multiply_reduce_fusion = (f32[8,512]{1,0:T(8,128)S(1)}, f32[8,512,512]{1,2,0:T(8,128)S(1)}) fusion(bf16[512,3,8,64]{0,3,2,1:T(8,128)(2,1)S(1)} %bitcast.90), kind=kOutput, calls=%fused_computation.2 | convolution fusion | flops 272625664 | bytes 9453568 | tf_op jit(solution)/shard_map/while/body/eval_jaxpr/qhd,khd->hqk/dot_general | solution.py:35
  8.9 1.4 %fusion.1 = f32[8,512]{1,0:T(8,128)S(1)} fusion(f32[8,512,512]{1,2,0:T(8,128)S(1)} %get-tuple-element.32, f32[8,512]{1,0:T(8,128)S(1)} %get-tuple-element.31), kind=kLoop, calls=%fused_computation.3 | loop fusion | flops 6287360 | bytes 8421376 | tf_op jit(solution)/shard_map/while/body/eval_jaxpr/reduce_sum | solution.py:39
  10.3 0.0 copy-start.3
  10.3 0.0 copy-start.6
  10.3 1.6 %divide_convert_fusion = bf16[512,8,64]{0,2,1:T(8,128)(2,1)S(1)} fusion(f32[8,512,512]{1,2,0:T(8,128)S(1)} %get-tuple-element.32, f32[8,512]{1,0:T(8,128)S(1)} %get-tuple-element.31, bf16[512,3,8,64]{0,3,2,1:T(8,128)(2,1)S(1)} %bitcast.91, f32[512,8]{0,1:T(8,128)S(1)} %bitcast.95), kind=kOutput, calls=%fused_computation.39 | convolution fusion | flops 275251200 | bytes 9469952 | tf_op jit(solution)/shard_map/while/body/eval_jaxpr/hqk,khd->qhd/dot_general | solution.py:40
  11.9 0.0 copy-done.3
  11.9 0.0 copy-done.6
  12.0 0.5 fusion.17
  12.4 0.8 copy.53
  13.2 0.5 broadcast.90
  13.8 3.8 %reduce.3 = bf16[512,512]{1,0:T(8,128)(2,1)S(1)} reduce(bf16[512,1,512]{2,1,0:T(2,128)(2,1)S(1)} %bitcast.92, bf16[]{:T(256)} %broadcast.90), dimensions={1}, to_apply=%bitcast.89.reduce_sub_computation | reduce | bytes 1048578
  17.6 1.0 reshape.81
  18.6 13.2 %all-to-all-start = ((bf16[64,2,2048]{2,1,0:T(2,128)(2,1)}), bf16[64,2,2048]{2,1,0:T(2,128)(2,1)S(1)}, u32[]{:S(2)}, u32[]{:S(2)}) async-start(bf16[64,2,2048]{2,1,0:T(2,128)(2,1)} %reshape.81), calls=%async_computation | async-start | bytes 1048576 | tf_op jit(solution)/shard_map/all_to_all | solution.py:100
  31.8 17.7 %all-to-all-done = bf16[64,2,2048]{2,1,0:T(2,128)(2,1)S(1)} async-done(((bf16[64,2,2048]{2,1,0:T(2,128)(2,1)}), bf16[64,2,2048]{2,1,0:T(2,128)(2,1)S(1)}, u32[]{:S(2)}, u32[]{:S(2)}) %all-to-all-start) | async-done | bytes 524320 | tf_op jit(solution)/shard_map/all_to_all | solution.py:100
  49.4 0.5 reshape.82
  50.0 0.0 copy-start.5
  50.0 1.6 %convert_reduce_fusion.1 = f32[512]{0:T(512)S(1)} fusion(bf16[512,1,512]{2,1,0:T(2,128)(2,1)S(1)} %reshape.82), kind=kLoop, calls=%fused_computation.55 | loop fusion | flops 523776 | bytes 526336 | tf_op jit(solution)/shard_map/while/body/eval_jaxpr/reduce_sum | solution.py:15
  51.6 1.1 %bitcast_convert_fusion = f32[1,512,512]{2,0,1:T(1,128)S(1)} fusion(bf16[512,1,512]{2,1,0:T(2,128)(2,1)S(1)} %reshape.82), kind=kLoop, calls=%fused_computation.61 | loop fusion | flops 262144 | bytes 1572864 | tf_op jit(solution)/shard_map/while/body/eval_jaxpr/convert_element_type | solution.py:77
  52.7 0.0 copy-start.1
  52.7 7.4 %multiply_reduce_fusion.1 = f32[512]{0:T(512)S(1)} fusion(f32[512]{0:T(512)S(1)} %broadcast_multiply_fusion, bf16[512,1,512]{2,1,0:T(2,128)(2,1)S(1)} %reshape.82), kind=kLoop, calls=%fused_computation.38 | loop fusion | flops 1048064 | bytes 528384 | tf_op jit(solution)/shard_map/while/body/eval_jaxpr/reduce_sum | solution.py:17
  60.2 0.0 copy-done.1
  60.2 0.0 copy-done.5
  60.2 1.0 convolution_convert_fusion
  61.2 3.2 %reshape.77 = bf16[64,8,3,8,64]{4,3,2,1,0:T(8,128)(2,1)} reshape(bf16[512,1536]{1,0:T(8,128)(2,1)S(1)} %convolution_convert_fusion) | data formatting | bytes 3145728 | tf_op jit(solution)/shard_map/while/body/eval_jaxpr/reshape | solution.py:27
  64.4 4.1 %fusion.41 = (bf16[64,8,1,8,64]{4,3,2,1,0:T(8,128)(2,1)}, bf16[64,8,1,8,64]{4,3,2,1,0:T(8,128)(2,1)S(1)}, bf16[64,8,1,8,64]{4,3,2,1,0:T(8,128)(2,1)}) fusion(bf16[64,8,3,8,64]{4,3,2,1,0:T(8,128)(2,1)} %reshape.77), kind=kLoop, calls=%fused_computation.59 | loop fusion | bytes 3145728 | tf_op jit(solution)/shard_map/while/body/eval_jaxpr/slice | solution.py:28
  68.5 2.0 %copy.34 = bf16[64,8,1,8,64]{0,4,3,1,2:T(8,128)(2,1)} copy(bf16[64,8,1,8,64]{4,3,2,1,0:T(8,128)(2,1)S(1)} %get-tuple-element.24) | data formatting | bytes 1048576
  70.5 0.0 copy-start.4
  70.5 4.7 %fusion.42 = (f32[8,8,64]{2,1,0:T(8,128)S(1)}, bf16[8,8,64,64]{2,3,1,0:T(8,128)(2,1)}) fusion(pred[64,64]{0,1:T(8,128)(4,1)S(1)} %iota_compare_fusion, bf16[64,8,1,8,64]{4,3,2,1,0:T(8,128)(2,1)} %get-tuple-element.30, bf16[64,8,1,8,64]{4,3,2,1,0:T(8,128)(2,1)} %get-tuple-element.23), kind=kOutput, calls=%fused_computation.60 | convolution fusion | flops 35127360 | bytes 1593344 | tf_op jit(solution)/shard_map/while/body/eval_jaxpr/sub | solution.py:64
  75.1 0.0 copy-done.4
  75.1 2.7 %fusion.7 = bf16[64,8,8,64]{0,3,2,1:T(8,128)(2,1)} fusion(bf16[64,8,1,8,64]{0,4,3,1,2:T(8,128)(2,1)S(1)} %copy-done.4, f32[64,8,8]{0,2,1:T(8,128)S(1)} %bitcast.97, bf16[8,8,64,64]{2,3,1,0:T(8,128)(2,1)} %get-tuple-element.34), kind=kOutput, calls=%fused_computation.11 | convolution fusion | flops 34078720 | bytes 1589248 | tf_op jit(solution)/shard_map/while/body/eval_jaxpr/chqk,kchd->qchd/dot_general | solution.py:66
  77.8 0.0 copy-start.2
  77.8 2.0 %copy.29 = bf16[64,8,512]{2,1,0:T(8,128)(2,1)S(1)} copy(bf16[64,8,512]{0,2,1:T(8,128)(2,1)} %bitcast.94) | data formatting | bytes 1048576 | tf_op jit(solution)/shard_map/while/body/eval_jaxpr/dot_general | solution.py:74
  79.8 0.0 copy-done.2
  79.9 1.5 %fusion.14 = bf16[64,8,512]{2,1,0:T(8,128)(2,1)S(1)} fusion(bf16[64,8,512]{2,1,0:T(8,128)(2,1)S(1)} %copy.29, f32[1,512,512]{2,0,1:T(1,128)S(1)} %copy-done.2, bf16[512,512]{1,0:T(8,128)(2,1)} %param.9), kind=kOutput, calls=%fused_computation.22 | convolution fusion | flops 268959744 | bytes 2621440 | tf_op jit(solution)/shard_map/while/body/eval_jaxpr/dot_general | solution.py:74
  81.3 23.2 %all_to_all.21 = bf16[64,8,512]{2,1,0:T(8,128)(2,1)S(1)} all-to-all(bf16[64,8,512]{2,1,0:T(8,128)(2,1)S(1)} %fusion.14), channel_id=1, replica_groups=mesh['patch'=8,'tm'=8,'subject'=4] {'patch','tm'}, dimensions={0} | all-to-all | bytes 1048576 | tf_op jit(solution)/shard_map/all_to_all | solution.py:102
  104.5 0.8 copy.55
  (5 shorter events, 0.0 us)
Async XLA Ops:
  0.0 2.7 %copy-start = (bf16[512,1536]{1,0:T(8,128)(2,1)S(1)}, bf16[512,1536]{1,0:T(8,128)(2,1)}, u32[]{:S(2)}) copy-start(bf16[512,1536]{1,0:T(8,128)(2,1)} %param.6) | copy-start | bytes 4718596
  10.3 1.6 %copy-start.3 = (bf16[1,512,512]{2,1,0:T(8,128)(2,1)S(1)}, bf16[1,512,512]{2,1,0:T(8,128)(2,1)}, u32[]{:S(2)}) copy-start(bf16[1,512,512]{2,1,0:T(8,128)(2,1)} %param.5) | copy-start | bytes 1572868
  10.3 1.6 %copy-start.6 = (bf16[512,512]{1,0:T(8,128)(2,1)S(1)}, bf16[512,512]{1,0:T(8,128)(2,1)}, u32[]{:S(2)}) copy-start(bf16[512,512]{1,0:T(8,128)(2,1)} %param.7) | copy-start | bytes 1572868
  18.6 30.8 %all-to-all-start = ((bf16[64,2,2048]{2,1,0:T(2,128)(2,1)}), bf16[64,2,2048]{2,1,0:T(2,128)(2,1)S(1)}, u32[]{:S(2)}, u32[]{:S(2)}) async-start(bf16[64,2,2048]{2,1,0:T(2,128)(2,1)} %reshape.81), calls=%async_computation | async-start | bytes 1048576 | tf_op jit(solution)/shard_map/all_to_all | solution.py:100
  50.0 10.2 %copy-start.5 = (bf16[512,1536]{1,0:T(8,128)(2,1)S(1)}, bf16[512,1536]{1,0:T(8,128)(2,1)}, u32[]{:S(2)}) copy-start(bf16[512,1536]{1,0:T(8,128)(2,1)} %param.8) | copy-start | bytes 4718596
  52.7 7.5 %copy-start.1 = (f32[1,512,512]{2,0,1:T(1,128)}, f32[1,512,512]{2,0,1:T(1,128)S(1)}, u32[]{:S(2)}) copy-start(f32[1,512,512]{2,0,1:T(1,128)S(1)} %bitcast_convert_fusion) | copy-start | bytes 3145732
  70.5 4.7 %copy-start.4 = (bf16[64,8,1,8,64]{0,4,3,1,2:T(8,128)(2,1)S(1)}, bf16[64,8,1,8,64]{0,4,3,1,2:T(8,128)(2,1)}, u32[]{:S(2)}) copy-start(bf16[64,8,1,8,64]{0,4,3,1,2:T(8,128)(2,1)} %copy.34) | copy-start | bytes 1572868
  77.8 2.0 %copy-start.2 = (f32[1,512,512]{2,0,1:T(1,128)S(1)}, f32[1,512,512]{2,0,1:T(1,128)}, u32[]{:S(2)}) copy-start(f32[1,512,512]{2,0,1:T(1,128)} %copy-done.1) | copy-start | bytes 3145732
where the time goes:
time: 106 us; the launch traced here: 105 us
  blocking collectives  23.2 us (22%)
  other arithmetic  18 us (17%)
  waiting for transfers between devices  17.7 us (17%)
  local copies, waits for them, and re-layouts  16.6 us (16%)
  matrix products  16.5 us (16%)
  starting transfers between devices  13.2 us (12%)
    all_to_all x1, blocking collectives, body(): lax.all_to_all(result, ('patch', 'tm'), split_axis=0, concat_axis=1, tile...  23.2 us
    all_to_all x1, waiting for transfers between devices, body(): lax.all_to_all(hidden, ('patch', 'tm'), split_axis=1, concat_axis=0, tile...  17.7 us
    all_to_all x1, starting transfers between devices, body(): lax.all_to_all(hidden, ('patch', 'tm'), split_axis=1, concat_axis=0, tile...  13.2 us
    reduce_sum x2, other arithmetic, layer_norm(): spread = jnp.mean(centered * centered, axis=-1, keepdims=True)  8.77 us
    unnamed x19, local copies, waits for them, and re-layouts  4.83 us
    sub x1, matrix products, causal_columns(): exp_terms = jnp.where(allowed, jnp.exp(masked - highest), 0.0)  4.68 us
    dot_general x2, matrix products, project_heads(): jnp.dot(normed.reshape(-1, model_width), qkv_weight, preferred_element_ty...  4.27 us
    slice x1, local copies, waits for them, and re-layouts, project_heads(): return (shaped[..., 0, :, :], shaped[..., 1, :, :], shaped[..., 2, :, :])  4.08 us
  transfers between devices with their start and end apart: 1, of which 1 were waited for; matrix products, arithmetic and copies ran while one was open for 0% of the time, Pallas kernels for 0%

commit v1 on v0

v1 whole, which is shorter than its diff:
```python
import jax
import jax.numpy as jnp
from jax import lax
from jax.experimental import pallas as pl
from jax.experimental.pallas import tpu as pltpu
from jax.sharding import PartitionSpec as P

HEADS = 8

epsilon = 1e-05
floor_score = -1e30


def _layer_norm(rows):
    width = rows.shape[-1]
    centre = jnp.sum(rows, axis=-1, keepdims=True) * (1.0 / width)
    centered = rows - centre
    spread = jnp.sum(centered * centered, axis=-1, keepdims=True) * (1.0 / width)
    return (centered * lax.rsqrt(spread + epsilon)).astype(jnp.bfloat16)


def _attention_block(x_ref, wqkv_ref, wout_ref, o_ref, packed_ref, attn_ref, mask_fn):
    rows = x_ref[...].astype(jnp.float32)
    width = rows.shape[-1]
    head_dim = width // HEADS
    normed = _layer_norm(rows)
    packed_ref[...] = jnp.dot(
        normed, wqkv_ref[...], preferred_element_type=jnp.float32
    ).astype(jnp.bfloat16)
    factor = head_dim ** (-0.5)
    n_rows = rows.shape[0]
    allowed = mask_fn(n_rows)
    lane = lax.broadcasted_iota(jnp.int32, (1, 2 * head_dim), 1)
    low = lane < head_dim
    for pair in range(HEADS // 2):
        cols = slice(pair * 2 * head_dim, (pair + 1) * 2 * head_dim)
        q2 = packed_ref[:, cols]
        k2 = packed_ref[:, width + cols.start : width + cols.stop]
        v2 = packed_ref[:, 2 * width + cols.start : 2 * width + cols.stop]
        halves = []
        for sel in (low, jnp.logical_not(low)):
            qh = jnp.where(sel, q2, jnp.zeros_like(q2))
            scores = (
                lax.dot_general(
                    qh, k2, (((1,), (1,)), ((), ())), preferred_element_type=jnp.float32
                )
                * factor
            )
            if allowed is not None:
                scores = jnp.where(allowed, scores, floor_score)
            highest = jnp.max(scores, axis=-1, keepdims=True)
            exp_terms = jnp.exp(scores - highest)
            if allowed is not None:
                exp_terms = jnp.where(allowed, exp_terms, 0.0)
            total = jnp.sum(exp_terms, axis=-1, keepdims=True)
            mixture = jnp.dot(
                exp_terms.astype(jnp.bfloat16), v2, preferred_element_type=jnp.float32
            )
            halves.append(mixture / total)
        attn_ref[:, cols] = jnp.where(low, halves[0], halves[1]).astype(jnp.bfloat16)
    update = jnp.dot(attn_ref[...], wout_ref[...], preferred_element_type=jnp.float32)
    o_ref[...] = (rows + update).astype(jnp.bfloat16)


def _no_mask(n_rows):
    return None


def _make_causal_mask(group):
    def mask_fn(n_rows):
        r_a = lax.broadcasted_iota(jnp.int32, (n_rows, n_rows), 0)
        r_b = lax.broadcasted_iota(jnp.int32, (n_rows, n_rows), 1)
        return (r_b <= r_a) & (jnp.bitwise_and(r_a - r_b, group - 1) == 0)

    return mask_fn


def _layer_call(rows, qkv_weight, out_weight, mask_fn):
    n_rows, width = rows.shape

    def kernel(x_ref, wqkv_ref, wout_ref, o_ref, packed_ref, attn_ref):
        _attention_block(x_ref, wqkv_ref, wout_ref, o_ref, packed_ref, attn_ref, mask_fn)

    vmem = pl.BlockSpec(memory_space=pltpu.VMEM)
    return pl.pallas_call(
        kernel,
        out_shape=jax.ShapeDtypeStruct((n_rows, width), jnp.bfloat16),
        in_specs=[vmem, vmem, vmem],
        out_specs=vmem,
        scratch_shapes=[
            pltpu.VMEM((n_rows, 3 * width), jnp.bfloat16),
            pltpu.VMEM((n_rows, width), jnp.bfloat16),
        ],
        compiler_params=pltpu.CompilerParams(vmem_limit_bytes=48 * 1024 * 1024),
    )(rows, qkv_weight, out_weight)


def body(frames_in, spatial_qkv, spatial_out, temporal_qkv, temporal_out):
    n_frames, n_patches, width = frames_in.shape
    hidden = jnp.stack(
        [_layer_call(frames_in[f], spatial_qkv, spatial_out, _no_mask) for f in range(n_frames)]
    )
    columns = lax.all_to_all(hidden, ("patch", "tm"), split_axis=1, concat_axis=0, tiled=True)
    frame_total, column_count, _ = columns.shape
    assert column_count & (column_count - 1) == 0
    result = _layer_call(
        columns.reshape(frame_total * column_count, width),
        temporal_qkv,
        temporal_out,
        _make_causal_mask(column_count),
    ).reshape(frame_total, column_count, width)
    return lax.all_to_all(result, ("patch", "tm"), split_axis=0, concat_axis=1, tiled=True)


def solution(mesh):
    in_specs = (P(("subject", "patch", "tm"), None, None), P(), P(), P(), P())
    out_specs = P(("subject", "patch", "tm"), None, None)
    return jax.shard_map(body, mesh=mesh, in_specs=in_specs, out_specs=out_specs, check_vma=False)
```

time: 106 us -> 76.9 us (0.73)
  blocking collectives: 23.2 us -> 53.9 us
  waiting for transfers between devices: 17.7 us -> 0 us
  matrix products: 16.5 us -> 0 us
  other arithmetic: 18 us -> 3.82 us
  starting transfers between devices: 13.2 us -> 0 us
  Pallas kernels: 0 us -> 9.03 us
  local copies, waits for them, and re-layouts: 16.6 us -> 9.71 us
    all_to_all x0 -> x1, blocking collectives: none -> 30.7 us  [body(): lax.all_to_all(hidden, ('patch', 'tm'), split_axis=1, concat_axis=0, tile...]
    all_to_all x1 -> x0, waiting for transfers between devices: 17.7 us -> none  [body(): lax.all_to_all(hidden, ('patch', 'tm'), split_axis=1, concat_axis=0, tile...]
    all_to_all x1 -> x0, starting transfers between devices: 13.2 us -> none  [body(): lax.all_to_all(hidden, ('patch', 'tm'), split_axis=1, concat_axis=0, tile...]
    reduce_sum x5 -> x0, other arithmetic: 13.1 us -> none  [the longest x2 8.77 us: layer_norm(): spread = jnp.mean(centered * centered, axis=-1, keepdims=True)]
    dot_general x7 -> x0, matrix products: 11.8 us -> none  [the longest x2 4.27 us: project_heads(): jnp.dot(normed.reshape(-1, model_width), qkv_weight, preferred_element_ty...]
    pallas_call x0 -> x2, Pallas kernels: none -> 9.03 us  [_layer_call(): pl.pallas_call(kernel, out_shape=jax.ShapeDtypeStruct((n_rows, width), jn...]
    sub x1 -> x0, matrix products: 4.68 us -> none  [causal_columns(): exp_terms = jnp.where(allowed, jnp.exp(masked - highest), 0.0)]
    slice x1 -> x0, local copies, waits for them, and re-layouts: 4.08 us -> none  [project_heads(): return (shaped[..., 0, :, :], shaped[..., 1, :, :], shaped[..., 2, :, :])]
  transfers between devices with their start and end apart: 1 -> 0, of which waited for: 1 -> 0; matrix products, arithmetic and copies ran while one was open for 0% -> 0% of each run, Pallas kernels for 0% -> 0%
where the time goes in v1:
time: 76.9 us; the launch traced here: 76.5 us
  blocking collectives  53.9 us (70%)
  local copies, waits for them, and re-layouts  9.71 us (13%)
  Pallas kernels  9.03 us (12%)
  other arithmetic  3.82 us (5%)
    all_to_all x1, blocking collectives, body(): lax.all_to_all(hidden, ('patch', 'tm'), split_axis=1, concat_axis=0, tile...  30.7 us
    all_to_all x1, blocking collectives, body(): lax.all_to_all(result, ('patch', 'tm'), split_axis=0, concat_axis=1, tile...  23.2 us
    pallas_call x2, Pallas kernels, _layer_call(): pl.pallas_call(kernel, out_shape=jax.ShapeDtypeStruct((n_rows, width), jn...  9.03 us
    unnamed x15, local copies, waits for them, and re-layouts  8.9 us
    unnamed x1, other arithmetic  3.82 us

profile of v1, /device:TPU:1, one launch (start us, length us, event | category | flops | bytes accessed | tf_op | source)
XLA Modules:
  0.0 76.5 jit_solution(9269289646545325092)
XLA Ops:
  0.0 0.0 copy-start
  0.0 1.4 %copy-done = bf16[512,1536]{1,0:T(8,128)(2,1)S(1)} copy-done((bf16[512,1536]{1,0:T(8,128)(2,1)S(1)}, bf16[512,1536]{1,0:T(8,128)(2,1)}, u32[]{:S(2)}) %copy-start) | copy-done | bytes 1572888
  1.4 0.0 copy-start.2
  1.4 1.0 %copy-done.2 = bf16[1,512,512]{2,1,0:T(8,128)(2,1)S(1)} copy-done((bf16[1,512,512]{2,1,0:T(8,128)(2,1)S(1)}, bf16[1,512,512]{2,1,0:T(8,128)(2,1)}, u32[]{:S(2)}) %copy-start.2) | copy-done | bytes 524312
  2.5 0.0 copy-start.3
  2.5 1.0 %copy-done.3 = bf16[512,512]{1,0:T(8,128)(2,1)S(1)} copy-done((bf16[512,512]{1,0:T(8,128)(2,1)S(1)}, bf16[512,512]{1,0:T(8,128)(2,1)}, u32[]{:S(2)}) %copy-start.3) | copy-done | bytes 524312
  3.5 4.4 %shard_map.55 = bf16[512,512]{1,0:T(8,128)(2,1)S(1)} custom-call(bf16[512,512]{1,0:T(8,128)(2,1)S(1)} %bitcast.14, bf16[512,1536]{1,0:T(8,128)(2,1)S(1)} %copy-done, bf16[512,512]{1,0:T(8,128)(2,1)S(1)} %copy-done.3), custom_call_target="tpu_custom_call" | custom-call | tf_op jit(solution)/shard_map/pallas_call | solution.py:85
  7.9 0.8 %copy.12 = bf16[1,512,512]{2,0,1:T(2,128)(2,1)S(1)} copy(bf16[1,512,512]{2,1,0:T(8,128)(2,1)S(1)} %bitcast.12) | data formatting | bytes 1048576 | tf_op jit(solution)/shard_map/stack | solution.py:100
  8.8 0.5 broadcast
  9.3 3.8 %reduce = bf16[512,512]{1,0:T(8,128)(2,1)S(1)} reduce(bf16[512,1,512]{2,1,0:T(2,128)(2,1)S(1)} %bitcast.16, bf16[]{:T(256)} %broadcast), dimensions={1}, to_apply=%bitcast.10.reduce_sub_computation | reduce | bytes 1048578
  13.1 0.2 reshape.15
  13.3 30.7 %all_to_all.21 = bf16[64,2,2048]{2,1,0:T(2,128)(2,1)} all-to-all(bf16[64,2,2048]{2,1,0:T(2,128)(2,1)S(1)} %reshape.15), channel_id=1, replica_groups=mesh['patch'=8,'tm'=8,'subject'=4] {'patch','tm'}, dimensions={0} | all-to-all | bytes 1048576 | tf_op jit(solution)/shard_map/all_to_all | solution.py:103
  44.0 0.0 copy-start.1
  44.0 0.0 copy-start.4
  44.1 3.8 %reshape.16 = bf16[512,1,512]{2,1,0:T(2,128)(2,1)S(1)} reshape(bf16[64,2,2048]{2,1,0:T(2,128)(2,1)} %all_to_all.21) | data formatting | bytes 1048576
  47.8 0.1 copy.11
  48.0 0.0 copy-done.1
  48.0 0.0 copy-done.4
  48.0 4.6 %shard_map.56 = bf16[512,512]{1,0:T(8,128)(2,1)S(1)} custom-call(bf16[512,512]{1,0:T(8,128)(2,1)S(1)} %bitcast.11, bf16[512,1536]{1,0:T(8,128)(2,1)S(1)} %copy-done.1, bf16[512,512]{1,0:T(8,128)(2,1)S(1)} %copy-done.4), custom_call_target="tpu_custom_call" | custom-call | tf_op jit(solution)/shard_map/pallas_call | solution.py:85
  52.6 23.2 %all_to_all.22 = bf16[64,8,512]{2,1,0:T(8,128)(2,1)S(1)} all-to-all(bf16[64,8,512]{2,1,0:T(8,128)(2,1)S(1)} %bitcast.13), channel_id=1, replica_groups=mesh['patch'=8,'tm'=8,'subject'=4] {'patch','tm'}, dimensions={0} | all-to-all | bytes 1048576 | tf_op jit(solution)/shard_map/all_to_all | solution.py:112
  75.8 0.8 %copy.14 = bf16[1,512,512]{2,1,0:T(8,128)(2,1)} copy(bf16[1,512,512]{2,1,0:T(8,128)(2,1)S(1)} %bitcast.17) | data formatting | bytes 1048576
Async XLA Ops:
  0.0 1.4 %copy-start = (bf16[512,1536]{1,0:T(8,128)(2,1)S(1)}, bf16[512,1536]{1,0:T(8,128)(2,1)}, u32[]{:S(2)}) copy-start(bf16[512,1536]{1,0:T(8,128)(2,1)} %wqkv_ref.2) | copy-start | bytes 4718596
  1.4 1.0 %copy-start.2 = (bf16[1,512,512]{2,1,0:T(8,128)(2,1)S(1)}, bf16[1,512,512]{2,1,0:T(8,128)(2,1)}, u32[]{:S(2)}) copy-start(bf16[1,512,512]{2,1,0:T(8,128)(2,1)} %param.5) | copy-start | bytes 1572868
  2.5 1.0 %copy-start.3 = (bf16[512,512]{1,0:T(8,128)(2,1)S(1)}, bf16[512,512]{1,0:T(8,128)(2,1)}, u32[]{:S(2)}) copy-start(bf16[512,512]{1,0:T(8,128)(2,1)} %wout_ref.2) | copy-start | bytes 1572868
  44.0 3.9 %copy-start.1 = (bf16[512,1536]{1,0:T(8,128)(2,1)S(1)}, bf16[512,1536]{1,0:T(8,128)(2,1)}, u32[]{:S(2)}) copy-start(bf16[512,1536]{1,0:T(8,128)(2,1)} %wqkv_ref.3) | copy-start | bytes 4718596
  44.0 3.9 %copy-start.4 = (bf16[512,512]{1,0:T(8,128)(2,1)S(1)}, bf16[512,512]{1,0:T(8,128)(2,1)}, u32[]{:S(2)}) copy-start(bf16[512,512]{1,0:T(8,128)(2,1)} %wout_ref.3) | copy-start | bytes 1572868

commit v2 on v1

--- a/solution.py
+++ b/solution.py
@@ -97,10 +97,16 @@
 
 def body(frames_in, spatial_qkv, spatial_out, temporal_qkv, temporal_out):
     n_frames, n_patches, width = frames_in.shape
-    hidden = jnp.stack(
-        [_layer_call(frames_in[f], spatial_qkv, spatial_out, _no_mask) for f in range(n_frames)]
+    assert n_frames == 1
+    group = lax.axis_size(("patch", "tm"))
+    hidden = _layer_call(frames_in[0], spatial_qkv, spatial_out, _no_mask)
+    columns = lax.all_to_all(
+        hidden.reshape(group, n_patches // group, width),
+        ("patch", "tm"),
+        split_axis=0,
+        concat_axis=0,
+        tiled=True,
     )
-    columns = lax.all_to_all(hidden, ("patch", "tm"), split_axis=1, concat_axis=0, tiled=True)
     frame_total, column_count, _ = columns.shape
     assert column_count & (column_count - 1) == 0
     result = _layer_call(

time: 76.9 us -> 67.4 us (0.88)
  local copies, waits for them, and re-layouts: 9.71 us -> 4.29 us
  other arithmetic: 3.82 us -> 0 us
    unnamed x15 -> x11, local copies, waits for them, and re-layouts: 8.9 us -> 4.29 us
    unnamed x1 -> x0, other arithmetic: 3.82 us -> none
    another operation x1 -> x0, local copies, waits for them, and re-layouts: 0.81 us -> none  [body(): jnp.stack([_layer_call(frames_in[f], spatial_qkv, spatial_out, _no_mask)...]
where the time goes in v2:
time: 67.4 us; the launch traced here: 67.1 us
  blocking collectives  53.8 us (80%)
  Pallas kernels  9.03 us (13%)
  local copies, waits for them, and re-layouts  4.29 us (6%)
    all_to_all x1, blocking collectives, body(): lax.all_to_all(hidden.reshape(group, n_patches // group, width), ('patch'...  30.6 us
    all_to_all x1, blocking collectives, body(): lax.all_to_all(result, ('patch', 'tm'), split_axis=0, concat_axis=1, tile...  23.2 us
    pallas_call x2, Pallas kernels, _layer_call(): pl.pallas_call(kernel, out_shape=jax.ShapeDtypeStruct((n_rows, width), jn...  9.03 us
    unnamed x11, local copies, waits for them, and re-layouts  4.29 us

profile of v2, /device:TPU:1, one launch (start us, length us, event | category | flops | bytes accessed | tf_op | source)
XLA Modules:
  0.0 67.1 jit_solution(1738876666753071892)
XLA Ops:
  0.0 0.0 copy-start
  0.0 1.4 %copy-done = bf16[512,1536]{1,0:T(8,128)(2,1)S(1)} copy-done((bf16[512,1536]{1,0:T(8,128)(2,1)S(1)}, bf16[512,1536]{1,0:T(8,128)(2,1)}, u32[]{:S(2)}) %copy-start) | copy-done | bytes 1572888
  1.4 0.0 copy-start.2
  1.4 1.0 %copy-done.2 = bf16[1,512,512]{2,1,0:T(8,128)(2,1)S(1)} copy-done((bf16[1,512,512]{2,1,0:T(8,128)(2,1)S(1)}, bf16[1,512,512]{2,1,0:T(8,128)(2,1)}, u32[]{:S(2)}) %copy-start.2) | copy-done | bytes 524312
  2.5 0.0 copy-start.3
  2.5 1.0 %copy-done.3 = bf16[512,512]{1,0:T(8,128)(2,1)S(1)} copy-done((bf16[512,512]{1,0:T(8,128)(2,1)S(1)}, bf16[512,512]{1,0:T(8,128)(2,1)}, u32[]{:S(2)}) %copy-start.3) | copy-done | bytes 524312
  3.5 0.0 copy-start.1
  3.5 0.0 copy-start.4
  3.5 4.4 %shard_map.55 = bf16[512,512]{1,0:T(8,128)(2,1)S(1)} custom-call(bf16[512,512]{1,0:T(8,128)(2,1)S(1)} %bitcast.8, bf16[512,1536]{1,0:T(8,128)(2,1)S(1)} %copy-done, bf16[512,512]{1,0:T(8,128)(2,1)S(1)} %copy-done.3), custom_call_target="tpu_custom_call" | custom-call | tf_op jit(solution)/shard_map/pallas_call | solution.py:85
  7.9 30.6 %all_to_all.17 = bf16[64,8,512]{2,1,0:T(8,128)(2,1)S(1)} all-to-all(bf16[64,8,512]{2,1,0:T(8,128)(2,1)S(1)} %bitcast.7), channel_id=1, replica_groups=mesh['patch'=8,'tm'=8,'subject'=4] {'patch','tm'}, dimensions={0} | all-to-all | bytes 1048576 | tf_op jit(solution)/shard_map/all_to_all | solution.py:103
  38.6 0.0 copy-done.1
  38.6 0.0 copy-done.4
  38.6 4.6 %shard_map.56 = bf16[512,512]{1,0:T(8,128)(2,1)S(1)} custom-call(bf16[512,512]{1,0:T(8,128)(2,1)S(1)} %bitcast.5, bf16[512,1536]{1,0:T(8,128)(2,1)S(1)} %copy-done.1, bf16[512,512]{1,0:T(8,128)(2,1)S(1)} %copy-done.4), custom_call_target="tpu_custom_call" | custom-call | tf_op jit(solution)/shard_map/pallas_call | solution.py:85
  43.2 23.2 %all_to_all.18 = bf16[64,8,512]{2,1,0:T(8,128)(2,1)S(1)} all-to-all(bf16[64,8,512]{2,1,0:T(8,128)(2,1)S(1)} %bitcast.6), channel_id=1, replica_groups=mesh['patch'=8,'tm'=8,'subject'=4] {'patch','tm'}, dimensions={0} | all-to-all | bytes 1048576 | tf_op jit(solution)/shard_map/all_to_all | solution.py:118
  66.3 0.8 %copy.7 = bf16[1,512,512]{2,1,0:T(8,128)(2,1)} copy(bf16[1,512,512]{2,1,0:T(8,128)(2,1)S(1)} %bitcast.9) | data formatting | bytes 1048576
Async XLA Ops:
  0.0 1.4 %copy-start = (bf16[512,1536]{1,0:T(8,128)(2,1)S(1)}, bf16[512,1536]{1,0:T(8,128)(2,1)}, u32[]{:S(2)}) copy-start(bf16[512,1536]{1,0:T(8,128)(2,1)} %wqkv_ref.2) | copy-start | bytes 4718596
  1.4 1.0 %copy-start.2 = (bf16[1,512,512]{2,1,0:T(8,128)(2,1)S(1)}, bf16[1,512,512]{2,1,0:T(8,128)(2,1)}, u32[]{:S(2)}) copy-start(bf16[1,512,512]{2,1,0:T(8,128)(2,1)} %param.5) | copy-start | bytes 1572868
  2.5 1.0 %copy-start.3 = (bf16[512,512]{1,0:T(8,128)(2,1)S(1)}, bf16[512,512]{1,0:T(8,128)(2,1)}, u32[]{:S(2)}) copy-start(bf16[512,512]{1,0:T(8,128)(2,1)} %wout_ref.2) | copy-start | bytes 1572868
  3.5 35.1 %copy-start.1 = (bf16[512,1536]{1,0:T(8,128)(2,1)S(1)}, bf16[512,1536]{1,0:T(8,128)(2,1)}, u32[]{:S(2)}) copy-start(bf16[512,1536]{1,0:T(8,128)(2,1)} %wqkv_ref.3) | copy-start | bytes 4718596
  3.5 35.1 %copy-start.4 = (bf16[512,512]{1,0:T(8,128)(2,1)S(1)}, bf16[512,512]{1,0:T(8,128)(2,1)}, u32[]{:S(2)}) copy-start(bf16[512,512]{1,0:T(8,128)(2,1)} %wout_ref.3) | copy-start | bytes 1572868

commit v3 on v2

--- a/solution.py
+++ b/solution.py
@@ -19,14 +19,17 @@
     return (centered * lax.rsqrt(spread + epsilon)).astype(jnp.bfloat16)
 
 
-def _attention_block(x_ref, wqkv_ref, wout_ref, o_ref, packed_ref, attn_ref, mask_fn):
+def _attention_block(x_ref, w_copies, wqkv_ref, wout_ref, o_ref, packed_ref, attn_ref, mask_fn):
     rows = x_ref[...].astype(jnp.float32)
     width = rows.shape[-1]
     head_dim = width // HEADS
     normed = _layer_norm(rows)
-    packed_ref[...] = jnp.dot(
-        normed, wqkv_ref[...], preferred_element_type=jnp.float32
-    ).astype(jnp.bfloat16)
+    for part in range(3):
+        w_copies[part].wait()
+        cols = slice(part * width, (part + 1) * width)
+        packed_ref[:, cols] = jnp.dot(
+            normed, wqkv_ref[:, cols], preferred_element_type=jnp.float32
+        ).astype(jnp.bfloat16)
     factor = head_dim ** (-0.5)
     n_rows = rows.shape[0]
     allowed = mask_fn(n_rows)
@@ -58,6 +61,7 @@
             )
             halves.append(mixture / total)
         attn_ref[:, cols] = jnp.where(low, halves[0], halves[1]).astype(jnp.bfloat16)
+    w_copies[3].wait()
     update = jnp.dot(attn_ref[...], wout_ref[...], preferred_element_type=jnp.float32)
     o_ref[...] = (rows + update).astype(jnp.bfloat16)
 
@@ -75,31 +79,59 @@
     return mask_fn
 
 
-def _layer_call(rows, qkv_weight, out_weight, mask_fn):
+def _layer_call(rows, qkv_weight, out_weight, mask_fn, rows_in_hbm):
     n_rows, width = rows.shape
 
-    def kernel(x_ref, wqkv_ref, wout_ref, o_ref, packed_ref, attn_ref):
-        _attention_block(x_ref, wqkv_ref, wout_ref, o_ref, packed_ref, attn_ref, mask_fn)
+    def kernel(x_in, wqkv_hbm, wout_hbm, o_ref, x_vmem, wqkv_ref, wout_ref, packed_ref, attn_ref, sems):
+        if rows_in_hbm:
+            x_copy = pltpu.make_async_copy(x_in, x_vmem, sems.at[4])
+            x_copy.start()
+        w_copies = [
+            pltpu.make_async_copy(
+                wqkv_hbm.at[:, pl.ds(part * width, width)],
+                wqkv_ref.at[:, pl.ds(part * width, width)],
+                sems.at[part],
+            )
+            for part in range(3)
+        ]
+        w_copies.append(pltpu.make_async_copy(wout_hbm, wout_ref, sems.at[3]))
+        for copy in w_copies:
+            copy.start()
+        if rows_in_hbm:
+            x_copy.wait()
+            x_ref = x_vmem
+        else:
+            x_ref = x_in
+        _attention_block(x_ref, w_copies, wqkv_ref, wout_ref, o_ref, packed_ref, attn_ref, mask_fn)
 
     vmem = pl.BlockSpec(memory_space=pltpu.VMEM)
+    hbm = pl.BlockSpec(memory_space=pltpu.HBM)
     return pl.pallas_call(
         kernel,
         out_shape=jax.ShapeDtypeStruct((n_rows, width), jnp.bfloat16),
-        in_specs=[vmem, vmem, vmem],
+        in_specs=[hbm if rows_in_hbm else vmem, hbm, hbm],
         out_specs=vmem,
         scratch_shapes=[
+            pltpu.VMEM((n_rows, width), jnp.bfloat16),
+            pltpu.VMEM((width, 3 * width), jnp.bfloat16),
+            pltpu.VMEM((width, width), jnp.bfloat16),
             pltpu.VMEM((n_rows, 3 * width), jnp.bfloat16),
             pltpu.VMEM((n_rows, width), jnp.bfloat16),
+            pltpu.SemaphoreType.DMA((5,)),
         ],
         compiler_params=pltpu.CompilerParams(vmem_limit_bytes=48 * 1024 * 1024),
-    )(rows, qkv_weight, out_weight)
+    )(
+        pltpu.with_memory_space_constraint(rows, pltpu.HBM) if rows_in_hbm else rows,
+        pltpu.with_memory_space_constraint(qkv_weight, pltpu.HBM),
+        pltpu.with_memory_space_constraint(out_weight, pltpu.HBM),
+    )
 
 
 def body(frames_in, spatial_qkv, spatial_out, temporal_qkv, temporal_out):
     n_frames, n_patches, width = frames_in.shape
     assert n_frames == 1
     group = lax.axis_size(("patch", "tm"))
-    hidden = _layer_call(frames_in[0], spatial_qkv, spatial_out, _no_mask)
+    hidden = _layer_call(frames_in[0], spatial_qkv, spatial_out, _no_mask, True)
     columns = lax.all_to_all(
         hidden.reshape(group, n_patches // group, width),
         ("patch", "tm"),
@@ -114,6 +146,7 @@
         temporal_qkv,
         temporal_out,
         _make_causal_mask(column_count),
+        False,
     ).reshape(frame_total, column_count, width)
     return lax.all_to_all(result, ("patch", "tm"), split_axis=0, concat_axis=1, tiled=True)
 

time: 67.4 us -> 67 us (level)
  local copies, waits for them, and re-layouts: 4.29 us -> 0.79 us
  Pallas kernels: 9.03 us -> 12.2 us
    unnamed x11 -> x1, local copies, waits for them, and re-layouts: 4.29 us -> 0.79 us
    pallas_call x2, Pallas kernels: 9.03 us -> 12.2 us  [_layer_call(): pl.pallas_call(kernel, out_shape=jax.ShapeDtypeStruct((n_rows, width), jn...]
where the time goes in v3:
time: 67 us; the launch traced here: 66.8 us
  blocking collectives  53.8 us (80%)
  Pallas kernels  12.2 us (18%)
  local copies, waits for them, and re-layouts  0.79 us (1%)
    all_to_all x1, blocking collectives, body(): lax.all_to_all(hidden.reshape(group, n_patches // group, width), ('patch'...  30.6 us
    all_to_all x1, blocking collectives, body(): lax.all_to_all(result, ('patch', 'tm'), split_axis=0, concat_axis=1, tile...  23.2 us
    pallas_call x2, Pallas kernels, _layer_call(): pl.pallas_call(kernel, out_shape=jax.ShapeDtypeStruct((n_rows, width), jn...  12.2 us

profile of v3, /device:TPU:1, one launch (start us, length us, event | category | flops | bytes accessed | tf_op | source)
XLA Modules:
  0.0 66.8 jit_solution(14836789979588076157)
XLA Ops:
  0.0 6.2 %shard_map.55 = bf16[512,512]{1,0:T(8,128)(2,1)S(1)} custom-call(bf16[512,512]{1,0:T(8,128)(2,1)} %bitcast.9, bf16[512,1536]{1,0:T(8,128)(2,1)} %wqkv_hbm.2, bf16[512,512]{1,0:T(8,128)(2,1)} %wout_hbm.2), custom_call_target="tpu_custom_call" | custom-call | tf_op jit(solution)/shard_map/pallas_call | solution.py:109
  6.2 30.6 %all_to_all.17 = bf16[64,8,512]{2,1,0:T(8,128)(2,1)S(1)} all-to-all(bf16[64,8,512]{2,1,0:T(8,128)(2,1)S(1)} %bitcast.7), channel_id=1, replica_groups=mesh['patch'=8,'tm'=8,'subject'=4] {'patch','tm'}, dimensions={0} | all-to-all | bytes 1048576 | tf_op jit(solution)/shard_map/all_to_all | solution.py:135
  36.8 6.1 %shard_map.56 = bf16[512,512]{1,0:T(8,128)(2,1)S(1)} custom-call(bf16[512,512]{1,0:T(8,128)(2,1)S(1)} %bitcast.5, bf16[512,1536]{1,0:T(8,128)(2,1)} %wqkv_hbm.3, bf16[512,512]{1,0:T(8,128)(2,1)} %wout_hbm.3), custom_call_target="tpu_custom_call" | custom-call | tf_op jit(solution)/shard_map/pallas_call | solution.py:109
  42.9 23.2 %all_to_all.18 = bf16[64,8,512]{2,1,0:T(8,128)(2,1)S(1)} all-to-all(bf16[64,8,512]{2,1,0:T(8,128)(2,1)S(1)} %bitcast.6), channel_id=1, replica_groups=mesh['patch'=8,'tm'=8,'subject'=4] {'patch','tm'}, dimensions={0} | all-to-all | bytes 1048576 | tf_op jit(solution)/shard_map/all_to_all | solution.py:151
  66.0 0.8 %copy.7 = bf16[1,512,512]{2,1,0:T(8,128)(2,1)} copy(bf16[1,512,512]{2,1,0:T(8,128)(2,1)S(1)} %bitcast.8) | data formatting | bytes 1048576

commit v4 on v3

--- a/solution.py
+++ b/solution.py
@@ -25,7 +25,8 @@
     head_dim = width // HEADS
     normed = _layer_norm(rows)
     for part in range(3):
-        w_copies[part].wait()
+        if w_copies is not None:
+            w_copies[part].wait()
         cols = slice(part * width, (part + 1) * width)
         packed_ref[:, cols] = jnp.dot(
             normed, wqkv_ref[:, cols], preferred_element_type=jnp.float32
@@ -61,7 +62,8 @@
             )
             halves.append(mixture / total)
         attn_ref[:, cols] = jnp.where(low, halves[0], halves[1]).astype(jnp.bfloat16)
-    w_copies[3].wait()
+    if w_copies is not None:
+        w_copies[3].wait()
     update = jnp.dot(attn_ref[...], wout_ref[...], preferred_element_type=jnp.float32)
     o_ref[...] = (rows + update).astype(jnp.bfloat16)
 
@@ -86,30 +88,33 @@
         if rows_in_hbm:
             x_copy = pltpu.make_async_copy(x_in, x_vmem, sems.at[4])
             x_copy.start()
-        w_copies = [
-            pltpu.make_async_copy(
-                wqkv_hbm.at[:, pl.ds(part * width, width)],
-                wqkv_ref.at[:, pl.ds(part * width, width)],
-                sems.at[part],
+        if rows_in_hbm:
+            w_copies = [
+                pltpu.make_async_copy(
+                    wqkv_hbm.at[:, pl.ds(part * width, width)],
+                    wqkv_ref.at[:, pl.ds(part * width, width)],
+                    sems.at[part],
+                )
+                for part in range(3)
+            ]
+            w_copies.append(pltpu.make_async_copy(wout_hbm, wout_ref, sems.at[3]))
+            for copy in w_copies:
+                copy.start()
+            x_copy.wait()
+            _attention_block(
+                x_vmem, w_copies, wqkv_ref, wout_ref, o_ref, packed_ref, attn_ref, mask_fn
             )
-            for part in range(3)
-        ]
-        w_copies.append(pltpu.make_async_copy(wout_hbm, wout_ref, sems.at[3]))
-        for copy in w_copies:
-            copy.start()
-        if rows_in_hbm:
-            x_copy.wait()
-            x_ref = x_vmem
         else:
-            x_ref = x_in
-        _attention_block(x_ref, w_copies, wqkv_ref, wout_ref, o_ref, packed_ref, attn_ref, mask_fn)
+            _attention_block(
+                x_in, None, wqkv_hbm, wout_hbm, o_ref, packed_ref, attn_ref, mask_fn
+            )
 
     vmem = pl.BlockSpec(memory_space=pltpu.VMEM)
     hbm = pl.BlockSpec(memory_space=pltpu.HBM)
     return pl.pallas_call(
         kernel,
         out_shape=jax.ShapeDtypeStruct((n_rows, width), jnp.bfloat16),
-        in_specs=[hbm if rows_in_hbm else vmem, hbm, hbm],
+        in_specs=[hbm, hbm, hbm] if rows_in_hbm else [vmem, vmem, vmem],
         out_specs=vmem,
         scratch_shapes=[
             pltpu.VMEM((n_rows, width), jnp.bfloat16),
@@ -122,8 +127,8 @@
         compiler_params=pltpu.CompilerParams(vmem_limit_bytes=48 * 1024 * 1024),
     )(
         pltpu.with_memory_space_constraint(rows, pltpu.HBM) if rows_in_hbm else rows,
-        pltpu.with_memory_space_constraint(qkv_weight, pltpu.HBM),
-        pltpu.with_memory_space_constraint(out_weight, pltpu.HBM),
+        pltpu.with_memory_space_constraint(qkv_weight, pltpu.HBM) if rows_in_hbm else qkv_weight,
+        pltpu.with_memory_space_constraint(out_weight, pltpu.HBM) if rows_in_hbm else out_weight,
     )
 
 

time: 67 us -> 65.7 us (0.981)
  Pallas kernels: 12.2 us -> 10.9 us
    pallas_call x2, Pallas kernels: 12.2 us -> 10.9 us  [_layer_call(): pl.pallas_call(kernel, out_shape=jax.ShapeDtypeStruct((n_rows, width), jn...]
where the time goes in v4:
time: 65.7 us; the launch traced here: 65.6 us
  blocking collectives  53.8 us (82%)
  Pallas kernels  10.9 us (17%)
  local copies, waits for them, and re-layouts  0.8 us (1%)
    all_to_all x1, blocking collectives, body(): lax.all_to_all(hidden.reshape(group, n_patches // group, width), ('patch'...  30.6 us
    all_to_all x1, blocking collectives, body(): lax.all_to_all(result, ('patch', 'tm'), split_axis=0, concat_axis=1, tile...  23.2 us
    pallas_call x2, Pallas kernels, _layer_call(): pl.pallas_call(kernel, out_shape=jax.ShapeDtypeStruct((n_rows, width), jn...  10.9 us

profile of v4, /device:TPU:1, one launch (start us, length us, event | category | flops | bytes accessed | tf_op | source)
XLA Modules:
  0.0 65.6 jit_solution(7491598249264046551)
XLA Ops:
  0.0 0.0 copy-start
  0.0 0.0 copy-start.1
  0.0 6.3 %shard_map.55 = bf16[512,512]{1,0:T(8,128)(2,1)S(1)} custom-call(bf16[512,512]{1,0:T(8,128)(2,1)} %bitcast.9, bf16[512,1536]{1,0:T(8,128)(2,1)} %wqkv_hbm.2, bf16[512,512]{1,0:T(8,128)(2,1)} %wout_hbm.2), custom_call_target="tpu_custom_call" | custom-call | tf_op jit(solution)/shard_map/pallas_call | solution.py:114
  6.3 30.6 %all_to_all.17 = bf16[64,8,512]{2,1,0:T(8,128)(2,1)S(1)} all-to-all(bf16[64,8,512]{2,1,0:T(8,128)(2,1)S(1)} %bitcast.7), channel_id=1, replica_groups=mesh['patch'=8,'tm'=8,'subject'=4] {'patch','tm'}, dimensions={0} | all-to-all | bytes 1048576 | tf_op jit(solution)/shard_map/all_to_all | solution.py:140
  36.9 0.0 copy-done
  36.9 0.0 copy-done.1
  36.9 4.6 %shard_map.56 = bf16[512,512]{1,0:T(8,128)(2,1)S(1)} custom-call(bf16[512,512]{1,0:T(8,128)(2,1)S(1)} %bitcast.5, bf16[512,1536]{1,0:T(8,128)(2,1)S(1)} %copy-done, bf16[512,512]{1,0:T(8,128)(2,1)S(1)} %copy-done.1), custom_call_target="tpu_custom_call" | custom-call | tf_op jit(solution)/shard_map/pallas_call | solution.py:114
  41.6 23.2 %all_to_all.18 = bf16[64,8,512]{2,1,0:T(8,128)(2,1)S(1)} all-to-all(bf16[64,8,512]{2,1,0:T(8,128)(2,1)S(1)} %bitcast.6), channel_id=1, replica_groups=mesh['patch'=8,'tm'=8,'subject'=4] {'patch','tm'}, dimensions={0} | all-to-all | bytes 1048576 | tf_op jit(solution)/shard_map/all_to_all | solution.py:156
  64.8 0.8 %copy.7 = bf16[1,512,512]{2,1,0:T(8,128)(2,1)} copy(bf16[1,512,512]{2,1,0:T(8,128)(2,1)S(1)} %bitcast.8) | data formatting | bytes 1048576
Async XLA Ops:
  0.0 36.9 %copy-start = (bf16[512,1536]{1,0:T(8,128)(2,1)S(1)}, bf16[512,1536]{1,0:T(8,128)(2,1)}, u32[]{:S(2)}) copy-start(bf16[512,1536]{1,0:T(8,128)(2,1)} %wqkv_hbm.3) | copy-start | bytes 4718596
  0.0 36.9 %copy-start.1 = (bf16[512,512]{1,0:T(8,128)(2,1)S(1)}, bf16[512,512]{1,0:T(8,128)(2,1)}, u32[]{:S(2)}) copy-start(bf16[512,512]{1,0:T(8,128)(2,1)} %wout_hbm.3) | copy-start | bytes 1572868

commit v5 on v4

--- a/solution.py
+++ b/solution.py
@@ -33,49 +33,53 @@
         ).astype(jnp.bfloat16)
     factor = head_dim ** (-0.5)
     n_rows = rows.shape[0]
-    allowed = mask_fn(n_rows)
     lane = lax.broadcasted_iota(jnp.int32, (1, 2 * head_dim), 1)
     low = lane < head_dim
+    if mask_fn is None:
+        blocks = [(0, n_rows, n_rows)]
+    else:
+        step = min(128, n_rows)
+        blocks = [(r0, step, r0 + step) for r0 in range(0, n_rows, step)]
     for pair in range(HEADS // 2):
         cols = slice(pair * 2 * head_dim, (pair + 1) * 2 * head_dim)
-        q2 = packed_ref[:, cols]
-        k2 = packed_ref[:, width + cols.start : width + cols.stop]
-        v2 = packed_ref[:, 2 * width + cols.start : 2 * width + cols.stop]
-        halves = []
-        for sel in (low, jnp.logical_not(low)):
-            qh = jnp.where(sel, q2, jnp.zeros_like(q2))
-            scores = (
-                lax.dot_general(
-                    qh, k2, (((1,), (1,)), ((), ())), preferred_element_type=jnp.float32
+        for r0, n_q, n_k in blocks:
+            q2 = packed_ref[r0 : r0 + n_q, cols]
+            k2 = packed_ref[:n_k, width + cols.start : width + cols.stop]
+            v2 = packed_ref[:n_k, 2 * width + cols.start : 2 * width + cols.stop]
+            allowed = None if mask_fn is None else mask_fn(r0, n_q, n_k)
+            halves = []
+            for sel in (low, jnp.logical_not(low)):
+                qh = jnp.where(sel, q2, jnp.zeros_like(q2))
+                scores = (
+                    lax.dot_general(
+                        qh, k2, (((1,), (1,)), ((), ())), preferred_element_type=jnp.float32
+                    )
+                    * factor
                 )
-                * factor
+                if allowed is not None:
+                    scores = jnp.where(allowed, scores, floor_score)
+                highest = jnp.max(scores, axis=-1, keepdims=True)
+                exp_terms = jnp.exp(scores - highest)
+                if allowed is not None:
+                    exp_terms = jnp.where(allowed, exp_terms, 0.0)
+                total = jnp.sum(exp_terms, axis=-1, keepdims=True)
+                mixture = jnp.dot(
+                    exp_terms.astype(jnp.bfloat16), v2, preferred_element_type=jnp.float32
+                )
+                halves.append(mixture * (1.0 / total))
+            attn_ref[r0 : r0 + n_q, cols] = jnp.where(low, halves[0], halves[1]).astype(
+                jnp.bfloat16
             )
-            if allowed is not None:
-                scores = jnp.where(allowed, scores, floor_score)
-            highest = jnp.max(scores, axis=-1, keepdims=True)
-            exp_terms = jnp.exp(scores - highest)
-            if allowed is not None:
-                exp_terms = jnp.where(allowed, exp_terms, 0.0)
-            total = jnp.sum(exp_terms, axis=-1, keepdims=True)
-            mixture = jnp.dot(
-                exp_terms.astype(jnp.bfloat16), v2, preferred_element_type=jnp.float32
-            )
-            halves.append(mixture / total)
-        attn_ref[:, cols] = jnp.where(low, halves[0], halves[1]).astype(jnp.bfloat16)
     if w_copies is not None:
         w_copies[3].wait()
     update = jnp.dot(attn_ref[...], wout_ref[...], preferred_element_type=jnp.float32)
     o_ref[...] = (rows + update).astype(jnp.bfloat16)
 
 
-def _no_mask(n_rows):
-    return None
-
-
 def _make_causal_mask(group):
-    def mask_fn(n_rows):
-        r_a = lax.broadcasted_iota(jnp.int32, (n_rows, n_rows), 0)
-        r_b = lax.broadcasted_iota(jnp.int32, (n_rows, n_rows), 1)
+    def mask_fn(r0, n_q, n_k):
+        r_a = lax.broadcasted_iota(jnp.int32, (n_q, n_k), 0) + r0
+        r_b = lax.broadcasted_iota(jnp.int32, (n_q, n_k), 1)
         return (r_b <= r_a) & (jnp.bitwise_and(r_a - r_b, group - 1) == 0)
 
     return mask_fn
@@ -136,7 +140,7 @@
     n_frames, n_patches, width = frames_in.shape
     assert n_frames == 1
     group = lax.axis_size(("patch", "tm"))
-    hidden = _layer_call(frames_in[0], spatial_qkv, spatial_out, _no_mask, True)
+    hidden = _layer_call(frames_in[0], spatial_qkv, spatial_out, None, True)
     columns = lax.all_to_all(
         hidden.reshape(group, n_patches // group, width),
         ("patch", "tm"),

time: 65.7 us -> 70.1 us (1.067)
  Pallas kernels: 10.9 us -> 15.3 us
    pallas_call x2, Pallas kernels: 10.9 us -> 15.3 us  [_layer_call(): pl.pallas_call(kernel, out_shape=jax.ShapeDtypeStruct((n_rows, width), jn...]
where the time goes in v5:
time: 70.1 us; the launch traced here: 69.9 us
  blocking collectives  53.8 us (77%)
  Pallas kernels  15.3 us (22%)
  local copies, waits for them, and re-layouts  0.8 us (1%)
    all_to_all x1, blocking collectives, body(): lax.all_to_all(hidden.reshape(group, n_patches // group, width), ('patch'...  30.6 us
    all_to_all x1, blocking collectives, body(): lax.all_to_all(result, ('patch', 'tm'), split_axis=0, concat_axis=1, tile...  23.2 us
    pallas_call x2, Pallas kernels, _layer_call(): pl.pallas_call(kernel, out_shape=jax.ShapeDtypeStruct((n_rows, width), jn...  15.3 us

profile of v5, /device:TPU:1, one launch (start us, length us, event | category | flops | bytes accessed | tf_op | source)
XLA Modules:
  0.0 69.9 jit_solution(17870865933347249082)
XLA Ops:
  0.0 0.0 copy-start
  0.0 0.0 copy-start.1
  0.0 6.3 %shard_map.55 = bf16[512,512]{1,0:T(8,128)(2,1)S(1)} custom-call(bf16[512,512]{1,0:T(8,128)(2,1)} %bitcast.9, bf16[512,1536]{1,0:T(8,128)(2,1)} %wqkv_hbm.2, bf16[512,512]{1,0:T(8,128)(2,1)} %wout_hbm.2), custom_call_target="tpu_custom_call" | custom-call | tf_op jit(solution)/shard_map/pallas_call | solution.py:118
  6.3 30.6 %all_to_all.17 = bf16[64,8,512]{2,1,0:T(8,128)(2,1)S(1)} all-to-all(bf16[64,8,512]{2,1,0:T(8,128)(2,1)S(1)} %bitcast.7), channel_id=1, replica_groups=mesh['patch'=8,'tm'=8,'subject'=4] {'patch','tm'}, dimensions={0} | all-to-all | bytes 1048576 | tf_op jit(solution)/shard_map/all_to_all | solution.py:144
  36.9 0.0 copy-done
  36.9 0.0 copy-done.1
  36.9 9.0 %shard_map.56 = bf16[512,512]{1,0:T(8,128)(2,1)S(1)} custom-call(bf16[512,512]{1,0:T(8,128)(2,1)S(1)} %bitcast.5, bf16[512,1536]{1,0:T(8,128)(2,1)S(1)} %copy-done, bf16[512,512]{1,0:T(8,128)(2,1)S(1)} %copy-done.1), custom_call_target="tpu_custom_call" | custom-call | tf_op jit(solution)/shard_map/pallas_call | solution.py:118
  45.9 23.2 %all_to_all.18 = bf16[64,8,512]{2,1,0:T(8,128)(2,1)S(1)} all-to-all(bf16[64,8,512]{2,1,0:T(8,128)(2,1)S(1)} %bitcast.6), channel_id=1, replica_groups=mesh['patch'=8,'tm'=8,'subject'=4] {'patch','tm'}, dimensions={0} | all-to-all | bytes 1048576 | tf_op jit(solution)/shard_map/all_to_all | solution.py:160
  69.1 0.8 %copy.7 = bf16[1,512,512]{2,1,0:T(8,128)(2,1)} copy(bf16[1,512,512]{2,1,0:T(8,128)(2,1)S(1)} %bitcast.8) | data formatting | bytes 1048576
Async XLA Ops:
  0.0 36.9 %copy-start = (bf16[512,1536]{1,0:T(8,128)(2,1)S(1)}, bf16[512,1536]{1,0:T(8,128)(2,1)}, u32[]{:S(2)}) copy-start(bf16[512,1536]{1,0:T(8,128)(2,1)} %wqkv_hbm.3) | copy-start | bytes 4718596
  0.0 36.9 %copy-start.1 = (bf16[512,512]{1,0:T(8,128)(2,1)S(1)}, bf16[512,512]{1,0:T(8,128)(2,1)}, u32[]{:S(2)}) copy-start(bf16[512,512]{1,0:T(8,128)(2,1)} %wout_hbm.3) | copy-start | bytes 1572868

commit v6 on v4

--- a/solution.py
+++ b/solution.py
@@ -6,6 +6,7 @@
 from jax.sharding import PartitionSpec as P
 
 HEADS = 8
+_GROUPS = 2
 
 epsilon = 1e-05
 floor_score = -1e30
@@ -24,19 +25,22 @@
     width = rows.shape[-1]
     head_dim = width // HEADS
     normed = _layer_norm(rows)
-    for part in range(3):
-        if w_copies is not None:
-            w_copies[part].wait()
-        cols = slice(part * width, (part + 1) * width)
-        packed_ref[:, cols] = jnp.dot(
-            normed, wqkv_ref[:, cols], preferred_element_type=jnp.float32
-        ).astype(jnp.bfloat16)
     factor = head_dim ** (-0.5)
     n_rows = rows.shape[0]
     allowed = mask_fn(n_rows)
     lane = lax.broadcasted_iota(jnp.int32, (1, 2 * head_dim), 1)
     low = lane < head_dim
+    group_width = width // _GROUPS
     for pair in range(HEADS // 2):
+        group = pair * 2 * head_dim // group_width
+        if pair * 2 * head_dim % group_width == 0:
+            for part in range(3):
+                if w_copies is not None:
+                    w_copies[group * 3 + part].wait()
+                cols = slice(part * width + group * group_width, part * width + (group + 1) * group_width)
+                packed_ref[:, cols] = jnp.dot(
+                    normed, wqkv_ref[:, cols], preferred_element_type=jnp.float32
+                ).astype(jnp.bfloat16)
         cols = slice(pair * 2 * head_dim, (pair + 1) * 2 * head_dim)
         q2 = packed_ref[:, cols]
         k2 = packed_ref[:, width + cols.start : width + cols.stop]
@@ -63,7 +67,7 @@
             halves.append(mixture / total)
         attn_ref[:, cols] = jnp.where(low, halves[0], halves[1]).astype(jnp.bfloat16)
     if w_copies is not None:
-        w_copies[3].wait()
+        w_copies[-1].wait()
     update = jnp.dot(attn_ref[...], wout_ref[...], preferred_element_type=jnp.float32)
     o_ref[...] = (rows + update).astype(jnp.bfloat16)
 
@@ -86,18 +90,20 @@
 
     def kernel(x_in, wqkv_hbm, wout_hbm, o_ref, x_vmem, wqkv_ref, wout_ref, packed_ref, attn_ref, sems):
         if rows_in_hbm:
-            x_copy = pltpu.make_async_copy(x_in, x_vmem, sems.at[4])
+            x_copy = pltpu.make_async_copy(x_in, x_vmem, sems.at[3 * _GROUPS + 1])
             x_copy.start()
         if rows_in_hbm:
+            group_width = width // _GROUPS
             w_copies = [
                 pltpu.make_async_copy(
-                    wqkv_hbm.at[:, pl.ds(part * width, width)],
-                    wqkv_ref.at[:, pl.ds(part * width, width)],
-                    sems.at[part],
+                    wqkv_hbm.at[:, pl.ds(part * width + group * group_width, group_width)],
+                    wqkv_ref.at[:, pl.ds(part * width + group * group_width, group_width)],
+                    sems.at[group * 3 + part],
                 )
+                for group in range(_GROUPS)
                 for part in range(3)
             ]
-            w_copies.append(pltpu.make_async_copy(wout_hbm, wout_ref, sems.at[3]))
+            w_copies.append(pltpu.make_async_copy(wout_hbm, wout_ref, sems.at[3 * _GROUPS]))
             for copy in w_copies:
                 copy.start()
             x_copy.wait()
@@ -122,7 +128,7 @@
             pltpu.VMEM((width, width), jnp.bfloat16),
             pltpu.VMEM((n_rows, 3 * width), jnp.bfloat16),
             pltpu.VMEM((n_rows, width), jnp.bfloat16),
-            pltpu.SemaphoreType.DMA((5,)),
+            pltpu.SemaphoreType.DMA((3 * _GROUPS + 2,)),
         ],
         compiler_params=pltpu.CompilerParams(vmem_limit_bytes=48 * 1024 * 1024),
     )(

time: 65.7 us -> 67 us (1.020)
  Pallas kernels: 10.9 us -> 12.2 us
    pallas_call x2, Pallas kernels: 10.9 us -> 12.2 us  [_layer_call(): pl.pallas_call(kernel, out_shape=jax.ShapeDtypeStruct((n_rows, width), jn...]
where the time goes in v6:
time: 67 us; the launch traced here: 66.8 us
  blocking collectives  53.8 us (80%)
  Pallas kernels  12.2 us (18%)
  local copies, waits for them, and re-layouts  0.8 us (1%)
    all_to_all x1, blocking collectives, body(): lax.all_to_all(hidden.reshape(group, n_patches // group, width), ('patch'...  30.6 us
    all_to_all x1, blocking collectives, body(): lax.all_to_all(result, ('patch', 'tm'), split_axis=0, concat_axis=1, tile...  23.2 us
    pallas_call x2, Pallas kernels, _layer_call(): pl.pallas_call(kernel, out_shape=jax.ShapeDtypeStruct((n_rows, width), jn...  12.2 us

profile of v6, /device:TPU:1, one launch (start us, length us, event | category | flops | bytes accessed | tf_op | source)
XLA Modules:
  0.0 66.8 jit_solution(12122927547491572949)
XLA Ops:
  0.0 0.0 copy-start
  0.0 0.0 copy-start.1
  0.0 7.2 %shard_map.55 = bf16[512,512]{1,0:T(8,128)(2,1)S(1)} custom-call(bf16[512,512]{1,0:T(8,128)(2,1)} %bitcast.9, bf16[512,1536]{1,0:T(8,128)(2,1)} %wqkv_hbm.2, bf16[512,512]{1,0:T(8,128)(2,1)} %wout_hbm.2), custom_call_target="tpu_custom_call" | custom-call | tf_op jit(solution)/shard_map/pallas_call | solution.py:120
  7.2 30.6 %all_to_all.17 = bf16[64,8,512]{2,1,0:T(8,128)(2,1)S(1)} all-to-all(bf16[64,8,512]{2,1,0:T(8,128)(2,1)S(1)} %bitcast.7), channel_id=1, replica_groups=mesh['patch'=8,'tm'=8,'subject'=4] {'patch','tm'}, dimensions={0} | all-to-all | bytes 1048576 | tf_op jit(solution)/shard_map/all_to_all | solution.py:146
  37.9 0.0 copy-done
  37.9 0.0 copy-done.1
  37.9 4.9 %shard_map.56 = bf16[512,512]{1,0:T(8,128)(2,1)S(1)} custom-call(bf16[512,512]{1,0:T(8,128)(2,1)S(1)} %bitcast.5, bf16[512,1536]{1,0:T(8,128)(2,1)S(1)} %copy-done, bf16[512,512]{1,0:T(8,128)(2,1)S(1)} %copy-done.1), custom_call_target="tpu_custom_call" | custom-call | tf_op jit(solution)/shard_map/pallas_call | solution.py:120
  42.8 23.2 %all_to_all.18 = bf16[64,8,512]{2,1,0:T(8,128)(2,1)S(1)} all-to-all(bf16[64,8,512]{2,1,0:T(8,128)(2,1)S(1)} %bitcast.6), channel_id=1, replica_groups=mesh['patch'=8,'tm'=8,'subject'=4] {'patch','tm'}, dimensions={0} | all-to-all | bytes 1048576 | tf_op jit(solution)/shard_map/all_to_all | solution.py:162
  66.0 0.8 %copy.7 = bf16[1,512,512]{2,1,0:T(8,128)(2,1)} copy(bf16[1,512,512]{2,1,0:T(8,128)(2,1)S(1)} %bitcast.8) | data formatting | bytes 1048576
Async XLA Ops:
  0.0 37.9 %copy-start = (bf16[512,1536]{1,0:T(8,128)(2,1)S(1)}, bf16[512,1536]{1,0:T(8,128)(2,1)}, u32[]{:S(2)}) copy-start(bf16[512,1536]{1,0:T(8,128)(2,1)} %wqkv_hbm.3) | copy-start | bytes 4718596
  0.0 37.9 %copy-start.1 = (bf16[512,512]{1,0:T(8,128)(2,1)S(1)}, bf16[512,512]{1,0:T(8,128)(2,1)}, u32[]{:S(2)}) copy-start(bf16[512,512]{1,0:T(8,128)(2,1)} %wout_hbm.3) | copy-start | bytes 1572868

commit v7 on v4

--- a/solution.py
+++ b/solution.py
@@ -62,6 +62,9 @@
             )
             halves.append(mixture / total)
         attn_ref[:, cols] = jnp.where(low, halves[0], halves[1]).astype(jnp.bfloat16)
+    if wout_ref is None:
+        o_ref[...] = attn_ref[...]
+        return
     if w_copies is not None:
         w_copies[3].wait()
     update = jnp.dot(attn_ref[...], wout_ref[...], preferred_element_type=jnp.float32)
@@ -106,7 +109,7 @@
             )
         else:
             _attention_block(
-                x_in, None, wqkv_hbm, wout_hbm, o_ref, packed_ref, attn_ref, mask_fn
+                x_in, None, wqkv_hbm, None, o_ref, packed_ref, attn_ref, mask_fn
             )
 
     vmem = pl.BlockSpec(memory_space=pltpu.VMEM)
@@ -132,6 +135,22 @@
     )
 
 
+def _project_call(hidden, attn, out_weight):
+    n_rows, width = hidden.shape
+
+    def kernel(h_ref, a_ref, w_ref, o_ref):
+        update = jnp.dot(a_ref[...], w_ref[...], preferred_element_type=jnp.float32)
+        o_ref[...] = (h_ref[...].astype(jnp.float32) + update).astype(jnp.bfloat16)
+
+    vmem = pl.BlockSpec(memory_space=pltpu.VMEM)
+    return pl.pallas_call(
+        kernel,
+        out_shape=jax.ShapeDtypeStruct((n_rows, width), jnp.bfloat16),
+        in_specs=[vmem, vmem, vmem],
+        out_specs=vmem,
+    )(hidden, attn, out_weight)
+
+
 def body(frames_in, spatial_qkv, spatial_out, temporal_qkv, temporal_out):
     n_frames, n_patches, width = frames_in.shape
     assert n_frames == 1
@@ -153,7 +172,8 @@
         _make_causal_mask(column_count),
         False,
     ).reshape(frame_total, column_count, width)
-    return lax.all_to_all(result, ("patch", "tm"), split_axis=0, concat_axis=1, tiled=True)
+    attn = lax.all_to_all(result, ("patch", "tm"), split_axis=0, concat_axis=1, tiled=True)
+    return _project_call(hidden, attn.reshape(n_patches, width), temporal_out)[None]
 
 
 def solution(mesh):

time: 65.7 us -> 67.5 us (1.027)
  Pallas kernels: 10.9 us -> 13.4 us
  local copies, waits for them, and re-layouts: 0.8 us -> 0.01 us
    pallas_call x0 -> x1, Pallas kernels: none -> 2.59 us  [_project_call(): pl.pallas_call(kernel, out_shape=jax.ShapeDtypeStruct((n_rows, width), jn...]
    unnamed x5 -> x6, local copies, waits for them, and re-layouts: 0.8 us -> 0.01 us
where the time goes in v7:
time: 67.5 us; the launch traced here: 67.3 us
  blocking collectives  53.9 us (80%)
  Pallas kernels  13.4 us (20%)
    all_to_all x1, blocking collectives, body(): lax.all_to_all(hidden.reshape(group, n_patches // group, width), ('patch'...  30.6 us
    all_to_all x1, blocking collectives, body(): lax.all_to_all(result, ('patch', 'tm'), split_axis=0, concat_axis=1, tile...  23.3 us
    pallas_call x2, Pallas kernels, _layer_call(): pl.pallas_call(kernel, out_shape=jax.ShapeDtypeStruct((n_rows, width), jn...  10.8 us
    pallas_call x1, Pallas kernels, _project_call(): pl.pallas_call(kernel, out_shape=jax.ShapeDtypeStruct((n_rows, width), jn...  2.59 us

profile of v7, /device:TPU:1, one launch (start us, length us, event | category | flops | bytes accessed | tf_op | source)
XLA Modules:
  0.0 67.3 jit_solution(15203709728219178875)
XLA Ops:
  0.0 0.0 copy-start.1
  0.0 0.0 copy-start.2
  0.0 6.3 %shard_map.55.h_ref = bf16[512,512]{1,0:T(8,128)(2,1)S(1)} custom-call(bf16[512,512]{1,0:T(8,128)(2,1)} %bitcast.10, bf16[512,1536]{1,0:T(8,128)(2,1)} %wqkv_hbm.2, bf16[512,512]{1,0:T(8,128)(2,1)} %wout_hbm.2), custom_call_target="tpu_custom_call" | custom-call | tf_op jit(solution)/shard_map/pallas_call | solution.py:117
  6.3 0.0 copy-start
  6.3 30.6 %all_to_all.14 = bf16[64,8,512]{2,1,0:T(8,128)(2,1)S(1)} all-to-all(bf16[64,8,512]{2,1,0:T(8,128)(2,1)S(1)} %bitcast.6), channel_id=1, replica_groups=mesh['patch'=8,'tm'=8,'subject'=4] {'patch','tm'}, dimensions={0} | all-to-all | bytes 1048576 | tf_op jit(solution)/shard_map/all_to_all | solution.py:159
  37.0 0.0 copy-done.1
  37.0 0.0 copy-done.2
  37.0 4.5 %shard_map.56 = bf16[512,512]{1,0:T(8,128)(2,1)S(1)} custom-call(bf16[512,512]{1,0:T(8,128)(2,1)S(1)} %bitcast.8, bf16[512,1536]{1,0:T(8,128)(2,1)S(1)} %copy-done.2, bf16[512,512]{1,0:T(8,128)(2,1)S(1)} %copy-done.1), custom_call_target="tpu_custom_call" | custom-call | tf_op jit(solution)/shard_map/pallas_call | solution.py:117
  41.4 0.0 copy-done
  41.5 23.3 %all_to_all.15 = bf16[64,8,512]{2,1,0:T(8,128)(2,1)} all-to-all(bf16[64,8,512]{2,1,0:T(8,128)(2,1)S(1)} %bitcast.7), channel_id=1, replica_groups=mesh['patch'=8,'tm'=8,'subject'=4] {'patch','tm'}, dimensions={0} | all-to-all | bytes 1048576 | tf_op jit(solution)/shard_map/all_to_all | solution.py:175
  64.7 2.6 %shard_map.57 = bf16[512,512]{1,0:T(8,128)(2,1)} custom-call(bf16[512,512]{1,0:T(8,128)(2,1)} %copy-done, bf16[512,512]{1,0:T(8,128)(2,1)} %bitcast.9, bf16[512,512]{1,0:T(8,128)(2,1)} %w_ref.1), custom_call_target="tpu_custom_call" | custom-call | tf_op jit(solution)/shard_map/pallas_call | solution.py:146
Async XLA Ops:
  0.0 37.0 %copy-start.1 = (bf16[512,512]{1,0:T(8,128)(2,1)S(1)}, bf16[512,512]{1,0:T(8,128)(2,1)}, u32[]{:S(2)}) copy-start(bf16[512,512]{1,0:T(8,128)(2,1)} %w_ref.1) | copy-start | bytes 1572868
  0.0 37.0 %copy-start.2 = (bf16[512,1536]{1,0:T(8,128)(2,1)S(1)}, bf16[512,1536]{1,0:T(8,128)(2,1)}, u32[]{:S(2)}) copy-start(bf16[512,1536]{1,0:T(8,128)(2,1)} %wqkv_hbm.3) | copy-start | bytes 4718596
  6.3 35.1 %copy-start = (bf16[512,512]{1,0:T(8,128)(2,1)}, bf16[512,512]{1,0:T(8,128)(2,1)S(1)}, u32[]{:S(2)}) copy-start(bf16[512,512]{1,0:T(8,128)(2,1)S(1)} %shard_map.55.h_ref) | copy-start | bytes 1572868

commit v8 on v4

--- a/solution.py
+++ b/solution.py
@@ -24,13 +24,12 @@
     width = rows.shape[-1]
     head_dim = width // HEADS
     normed = _layer_norm(rows)
-    for part in range(3):
-        if w_copies is not None:
+    if w_copies is not None:
+        for part in range(3):
             w_copies[part].wait()
-        cols = slice(part * width, (part + 1) * width)
-        packed_ref[:, cols] = jnp.dot(
-            normed, wqkv_ref[:, cols], preferred_element_type=jnp.float32
-        ).astype(jnp.bfloat16)
+    packed_ref[...] = jnp.dot(
+        normed, wqkv_ref[...], preferred_element_type=jnp.float32
+    ).astype(jnp.bfloat16)
     factor = head_dim ** (-0.5)
     n_rows = rows.shape[0]
     allowed = mask_fn(n_rows)

time: 65.7 us -> 65.5 us (level)
  no operation moved by 1% of the time
where the time goes in v8:
time: 65.5 us; the launch traced here: 65.4 us
  blocking collectives  53.8 us (82%)
  Pallas kernels  10.8 us (16%)
  local copies, waits for them, and re-layouts  0.8 us (1%)
    all_to_all x1, blocking collectives, body(): lax.all_to_all(hidden.reshape(group, n_patches // group, width), ('patch'...  30.6 us
    all_to_all x1, blocking collectives, body(): lax.all_to_all(result, ('patch', 'tm'), split_axis=0, concat_axis=1, tile...  23.2 us
    pallas_call x2, Pallas kernels, _layer_call(): pl.pallas_call(kernel, out_shape=jax.ShapeDtypeStruct((n_rows, width), jn...  10.8 us

profile of v8, /device:TPU:1, one launch (start us, length us, event | category | flops | bytes accessed | tf_op | source)
XLA Modules:
  0.0 65.4 jit_solution(15152548275094084614)
XLA Ops:
  0.0 0.0 copy-start
  0.0 0.0 copy-start.1
  0.0 6.1 %shard_map.55 = bf16[512,512]{1,0:T(8,128)(2,1)S(1)} custom-call(bf16[512,512]{1,0:T(8,128)(2,1)} %bitcast.9, bf16[512,1536]{1,0:T(8,128)(2,1)} %wqkv_hbm.2, bf16[512,512]{1,0:T(8,128)(2,1)} %wout_hbm.2), custom_call_target="tpu_custom_call" | custom-call | tf_op jit(solution)/shard_map/pallas_call | solution.py:113
  6.1 30.6 %all_to_all.17 = bf16[64,8,512]{2,1,0:T(8,128)(2,1)S(1)} all-to-all(bf16[64,8,512]{2,1,0:T(8,128)(2,1)S(1)} %bitcast.7), channel_id=1, replica_groups=mesh['patch'=8,'tm'=8,'subject'=4] {'patch','tm'}, dimensions={0} | all-to-all | bytes 1048576 | tf_op jit(solution)/shard_map/all_to_all | solution.py:139
  36.8 0.0 copy-done
  36.8 0.0 copy-done.1
  36.8 4.6 %shard_map.56 = bf16[512,512]{1,0:T(8,128)(2,1)S(1)} custom-call(bf16[512,512]{1,0:T(8,128)(2,1)S(1)} %bitcast.5, bf16[512,1536]{1,0:T(8,128)(2,1)S(1)} %copy-done, bf16[512,512]{1,0:T(8,128)(2,1)S(1)} %copy-done.1), custom_call_target="tpu_custom_call" | custom-call | tf_op jit(solution)/shard_map/pallas_call | solution.py:113
  41.4 23.2 %all_to_all.18 = bf16[64,8,512]{2,1,0:T(8,128)(2,1)S(1)} all-to-all(bf16[64,8,512]{2,1,0:T(8,128)(2,1)S(1)} %bitcast.6), channel_id=1, replica_groups=mesh['patch'=8,'tm'=8,'subject'=4] {'patch','tm'}, dimensions={0} | all-to-all | bytes 1048576 | tf_op jit(solution)/shard_map/all_to_all | solution.py:155
  64.6 0.8 %copy.7 = bf16[1,512,512]{2,1,0:T(8,128)(2,1)} copy(bf16[1,512,512]{2,1,0:T(8,128)(2,1)S(1)} %bitcast.8) | data formatting | bytes 1048576
Async XLA Ops:
  0.0 36.8 %copy-start = (bf16[512,1536]{1,0:T(8,128)(2,1)S(1)}, bf16[512,1536]{1,0:T(8,128)(2,1)}, u32[]{:S(2)}) copy-start(bf16[512,1536]{1,0:T(8,128)(2,1)} %wqkv_hbm.3) | copy-start | bytes 4718596
  0.0 36.8 %copy-start.1 = (bf16[512,512]{1,0:T(8,128)(2,1)S(1)}, bf16[512,512]{1,0:T(8,128)(2,1)}, u32[]{:S(2)}) copy-start(bf16[512,512]{1,0:T(8,128)(2,1)} %wout_hbm.3) | copy-start | bytes 1572868

commit v9 on v2

--- a/solution.py
+++ b/solution.py
@@ -19,11 +19,18 @@
     return (centered * lax.rsqrt(spread + epsilon)).astype(jnp.bfloat16)
 
 
-def _attention_block(x_ref, wqkv_ref, wout_ref, o_ref, packed_ref, attn_ref, mask_fn):
+def _attention_block(
+    x_ref, w_copies, wqkv_ref, wout_ref, o_ref, packed_ref, attn_ref, mask_fn, after_qkv=None
+):
     rows = x_ref[...].astype(jnp.float32)
     width = rows.shape[-1]
     head_dim = width // HEADS
     normed = _layer_norm(rows)
+    if w_copies is not None:
+        for part in range(3):
+            w_copies[part].wait()
+    if after_qkv is not None:
+        after_qkv.start()
     packed_ref[...] = jnp.dot(
         normed, wqkv_ref[...], preferred_element_type=jnp.float32
     ).astype(jnp.bfloat16)
@@ -58,8 +65,25 @@
             )
             halves.append(mixture / total)
         attn_ref[:, cols] = jnp.where(low, halves[0], halves[1]).astype(jnp.bfloat16)
+    if w_copies is not None:
+        w_copies[3].wait()
     update = jnp.dot(attn_ref[...], wout_ref[...], preferred_element_type=jnp.float32)
     o_ref[...] = (rows + update).astype(jnp.bfloat16)
+    if after_qkv is not None:
+        after_qkv.wait()
+
+
+class _Pair:
+    def __init__(self, copies):
+        self.copies = copies
+
+    def start(self):
+        for c in self.copies:
+            c.start()
+
+    def wait(self):
+        for c in self.copies:
+            c.wait()
 
 
 def _no_mask(n_rows):
@@ -75,11 +99,61 @@
     return mask_fn
 
 
-def _layer_call(rows, qkv_weight, out_weight, mask_fn):
+def _spatial_call(rows, qkv_weight, out_weight, next_qkv, next_out):
     n_rows, width = rows.shape
 
-    def kernel(x_ref, wqkv_ref, wout_ref, o_ref, packed_ref, attn_ref):
-        _attention_block(x_ref, wqkv_ref, wout_ref, o_ref, packed_ref, attn_ref, mask_fn)
+    def kernel(x_in, wqkv_hbm, wout_hbm, nqkv_hbm, nout_hbm, o_ref, nqkv_ref, nout_ref,
+               x_vmem, wqkv_ref, wout_ref, packed_ref, attn_ref, sems):
+        x_copy = pltpu.make_async_copy(x_in, x_vmem, sems.at[4])
+        x_copy.start()
+        w_copies = [
+            pltpu.make_async_copy(
+                wqkv_hbm.at[:, pl.ds(part * width, width)],
+                wqkv_ref.at[:, pl.ds(part * width, width)],
+                sems.at[part],
+            )
+            for part in range(3)
+        ]
+        w_copies.append(pltpu.make_async_copy(wout_hbm, wout_ref, sems.at[3]))
+        for copy in w_copies:
+            copy.start()
+        after = _Pair([
+            pltpu.make_async_copy(nqkv_hbm, nqkv_ref, sems.at[5]),
+            pltpu.make_async_copy(nout_hbm, nout_ref, sems.at[6]),
+        ])
+        x_copy.wait()
+        _attention_block(
+            x_vmem, w_copies, wqkv_ref, wout_ref, o_ref, packed_ref, attn_ref, _no_mask, after
+        )
+
+    vmem = pl.BlockSpec(memory_space=pltpu.VMEM)
+    hbm = pl.BlockSpec(memory_space=pltpu.HBM)
+    return pl.pallas_call(
+        kernel,
+        out_shape=(
+            jax.ShapeDtypeStruct((n_rows, width), jnp.bfloat16),
+            jax.ShapeDtypeStruct(next_qkv.shape, next_qkv.dtype),
+            jax.ShapeDtypeStruct(next_out.shape, next_out.dtype),
+        ),
+        in_specs=[hbm] * 5,
+        out_specs=(vmem, vmem, vmem),
+        scratch_shapes=[
+            pltpu.VMEM((n_rows, width), jnp.bfloat16),
+            pltpu.VMEM((width, 3 * width), jnp.bfloat16),
+            pltpu.VMEM((width, width), jnp.bfloat16),
+            pltpu.VMEM((n_rows, 3 * width), jnp.bfloat16),
+            pltpu.VMEM((n_rows, width), jnp.bfloat16),
+            pltpu.SemaphoreType.DMA((7,)),
+        ],
+        compiler_params=pltpu.CompilerParams(vmem_limit_bytes=48 * 1024 * 1024),
+    )(*[pltpu.with_memory_space_constraint(a, pltpu.HBM) for a in (rows, qkv_weight, out_weight, next_qkv, next_out)])
+
+
+def _temporal_call(rows, qkv_weight, out_weight, mask_fn):
+    n_rows, width = rows.shape
+
+    def kernel(x_in, wqkv_in, wout_in, o_ref, packed_ref, attn_ref):
+        _attention_block(x_in, None, wqkv_in, wout_in, o_ref, packed_ref, attn_ref, mask_fn)
 
     vmem = pl.BlockSpec(memory_space=pltpu.VMEM)
     return pl.pallas_call(
@@ -99,7 +173,9 @@
     n_frames, n_patches, width = frames_in.shape
     assert n_frames == 1
     group = lax.axis_size(("patch", "tm"))
-    hidden = _layer_call(frames_in[0], spatial_qkv, spatial_out, _no_mask)
+    hidden, t_qkv, t_out = _spatial_call(
+        frames_in[0], spatial_qkv, spatial_out, temporal_qkv, temporal_out
+    )
     columns = lax.all_to_all(
         hidden.reshape(group, n_patches // group, width),
         ("patch", "tm"),
@@ -109,10 +185,10 @@
     )
     frame_total, column_count, _ = columns.shape
     assert column_count & (column_count - 1) == 0
-    result = _layer_call(
+    result = _temporal_call(
         columns.reshape(frame_total * column_count, width),
-        temporal_qkv,
-        temporal_out,
+        t_qkv,
+        t_out,
         _make_causal_mask(column_count),
     ).reshape(frame_total, column_count, width)
     return lax.all_to_all(result, ("patch", "tm"), split_axis=0, concat_axis=1, tiled=True)

time: 67.4 us -> 65.4 us (0.970)
  local copies, waits for them, and re-layouts: 4.29 us -> 0.79 us
  Pallas kernels: 9.03 us -> 10.6 us
    unnamed x11 -> x1, local copies, waits for them, and re-layouts: 4.29 us -> 0.79 us
    pallas_call x2, Pallas kernels: 9.03 us -> 10.6 us  [the longest x1 5.99 us: _spatial_call(): pl.pallas_call(kernel, out_shape=(jax.ShapeDtypeStruct((n_rows, width), j...]
where the time goes in v9:
time: 65.4 us; the launch traced here: 65.2 us
  blocking collectives  53.8 us (82%)
  Pallas kernels  10.6 us (16%)
  local copies, waits for them, and re-layouts  0.79 us (1%)
    all_to_all x1, blocking collectives, body(): lax.all_to_all(hidden.reshape(group, n_patches // group, width), ('patch'...  30.6 us
    all_to_all x1, blocking collectives, body(): lax.all_to_all(result, ('patch', 'tm'), split_axis=0, concat_axis=1, tile...  23.2 us
    pallas_call x1, Pallas kernels, _spatial_call(): pl.pallas_call(kernel, out_shape=(jax.ShapeDtypeStruct((n_rows, width), j...  5.99 us
    pallas_call x1, Pallas kernels, _temporal_call(): pl.pallas_call(kernel, out_shape=jax.ShapeDtypeStruct((n_rows, width), jn...  4.58 us

profile of v9, /device:TPU:1, one launch (start us, length us, event | category | flops | bytes accessed | tf_op | source)
XLA Modules:
  0.0 65.2 jit_solution(11651052213252260068)
XLA Ops:
  0.0 6.0 %shard_map.55 = (bf16[512,512]{1,0:T(8,128)(2,1)S(1)}, bf16[512,1536]{1,0:T(8,128)(2,1)S(1)}, bf16[512,512]{1,0:T(8,128)(2,1)S(1)}) custom-call(bf16[512,512]{1,0:T(8,128)(2,1)} %bitcast.9, bf16[512,1536]{1,0:T(8,128)(2,1)} %wqkv_hbm.1, bf16[512,512]{1,0:T(8,128)(2,1)} %wout_hbm.1, bf16[512,1536]{1,0:T(8,128)(2,1)} %nqkv_hbm.1, bf16[512,512]{1,0:T(8,128)(2,1)} %nout_hbm.1), custom_call_target="tpu_custom_call" | custom-call | tf_op jit(solution)/shard_map/pallas_call | solution.py:131
  6.0 30.6 %all_to_all.17 = bf16[64,8,512]{2,1,0:T(8,128)(2,1)S(1)} all-to-all(bf16[64,8,512]{2,1,0:T(8,128)(2,1)S(1)} %bitcast.7), channel_id=1, replica_groups=mesh['patch'=8,'tm'=8,'subject'=4] {'patch','tm'}, dimensions={0} | all-to-all | bytes 1048576 | tf_op jit(solution)/shard_map/all_to_all | solution.py:179
  36.6 4.6 %shard_map.56 = bf16[512,512]{1,0:T(8,128)(2,1)S(1)} custom-call(bf16[512,512]{1,0:T(8,128)(2,1)S(1)} %bitcast.5, bf16[512,1536]{1,0:T(8,128)(2,1)S(1)} %get-tuple-element.9.wqkv_in, bf16[512,512]{1,0:T(8,128)(2,1)S(1)} %get-tuple-element.10.wout_in), custom_call_target="tpu_custom_call" | custom-call | tf_op jit(solution)/shard_map/pallas_call | solution.py:159
  41.2 23.2 %all_to_all.18 = bf16[64,8,512]{2,1,0:T(8,128)(2,1)S(1)} all-to-all(bf16[64,8,512]{2,1,0:T(8,128)(2,1)S(1)} %bitcast.6), channel_id=1, replica_groups=mesh['patch'=8,'tm'=8,'subject'=4] {'patch','tm'}, dimensions={0} | all-to-all | bytes 1048576 | tf_op jit(solution)/shard_map/all_to_all | solution.py:194
  64.4 0.8 %copy.7 = bf16[1,512,512]{2,1,0:T(8,128)(2,1)} copy(bf16[1,512,512]{2,1,0:T(8,128)(2,1)S(1)} %bitcast.8) | data formatting | bytes 1048576

commit v10 on v9

--- a/solution.py
+++ b/solution.py
@@ -70,7 +70,8 @@
     update = jnp.dot(attn_ref[...], wout_ref[...], preferred_element_type=jnp.float32)
     o_ref[...] = (rows + update).astype(jnp.bfloat16)
     if after_qkv is not None:
-        after_qkv.wait()
+        for copy in after_qkv.copies[1:]:
+            copy.wait()
 
 
 class _Pair:
@@ -115,9 +116,10 @@
             for part in range(3)
         ]
         w_copies.append(pltpu.make_async_copy(wout_hbm, wout_ref, sems.at[3]))
-        for copy in w_copies:
+        for copy in w_copies[:3]:
             copy.start()
         after = _Pair([
+            w_copies[3],
             pltpu.make_async_copy(nqkv_hbm, nqkv_ref, sems.at[5]),
             pltpu.make_async_copy(nout_hbm, nout_ref, sems.at[6]),
         ])

time: 65.4 us -> 65.4 us (level)
  no operation moved by 1% of the time
where the time goes in v10:
time: 65.4 us; the launch traced here: 65.2 us
  blocking collectives  53.8 us (82%)
  Pallas kernels  10.6 us (16%)
  local copies, waits for them, and re-layouts  0.79 us (1%)
    all_to_all x1, blocking collectives, body(): lax.all_to_all(hidden.reshape(group, n_patches // group, width), ('patch'...  30.6 us
    all_to_all x1, blocking collectives, body(): lax.all_to_all(result, ('patch', 'tm'), split_axis=0, concat_axis=1, tile...  23.2 us
    pallas_call x1, Pallas kernels, _spatial_call(): pl.pallas_call(kernel, out_shape=(jax.ShapeDtypeStruct((n_rows, width), j...  5.99 us
    pallas_call x1, Pallas kernels, _temporal_call(): pl.pallas_call(kernel, out_shape=jax.ShapeDtypeStruct((n_rows, width), jn...  4.58 us

profile of v10, /device:TPU:1, one launch (start us, length us, event | category | flops | bytes accessed | tf_op | source)
XLA Modules:
  0.0 65.2 jit_solution(10200981241288133570)
XLA Ops:
  0.0 6.0 %shard_map.55 = (bf16[512,512]{1,0:T(8,128)(2,1)S(1)}, bf16[512,1536]{1,0:T(8,128)(2,1)S(1)}, bf16[512,512]{1,0:T(8,128)(2,1)S(1)}) custom-call(bf16[512,512]{1,0:T(8,128)(2,1)} %bitcast.9, bf16[512,1536]{1,0:T(8,128)(2,1)} %wqkv_hbm.1, bf16[512,512]{1,0:T(8,128)(2,1)} %wout_hbm.1, bf16[512,1536]{1,0:T(8,128)(2,1)} %nqkv_hbm.1, bf16[512,512]{1,0:T(8,128)(2,1)} %nout_hbm.1), custom_call_target="tpu_custom_call" | custom-call | tf_op jit(solution)/shard_map/pallas_call | solution.py:133
  6.0 30.6 %all_to_all.17 = bf16[64,8,512]{2,1,0:T(8,128)(2,1)S(1)} all-to-all(bf16[64,8,512]{2,1,0:T(8,128)(2,1)S(1)} %bitcast.7), channel_id=1, replica_groups=mesh['patch'=8,'tm'=8,'subject'=4] {'patch','tm'}, dimensions={0} | all-to-all | bytes 1048576 | tf_op jit(solution)/shard_map/all_to_all | solution.py:181
  36.6 4.6 %shard_map.56 = bf16[512,512]{1,0:T(8,128)(2,1)S(1)} custom-call(bf16[512,512]{1,0:T(8,128)(2,1)S(1)} %bitcast.5, bf16[512,1536]{1,0:T(8,128)(2,1)S(1)} %get-tuple-element.9.wqkv_in, bf16[512,512]{1,0:T(8,128)(2,1)S(1)} %get-tuple-element.10.wout_in), custom_call_target="tpu_custom_call" | custom-call | tf_op jit(solution)/shard_map/pallas_call | solution.py:161
  41.2 23.2 %all_to_all.18 = bf16[64,8,512]{2,1,0:T(8,128)(2,1)S(1)} all-to-all(bf16[64,8,512]{2,1,0:T(8,128)(2,1)S(1)} %bitcast.6), channel_id=1, replica_groups=mesh['patch'=8,'tm'=8,'subject'=4] {'patch','tm'}, dimensions={0} | all-to-all | bytes 1048576 | tf_op jit(solution)/shard_map/all_to_all | solution.py:196
  64.4 0.8 %copy.7 = bf16[1,512,512]{2,1,0:T(8,128)(2,1)} copy(bf16[1,512,512]{2,1,0:T(8,128)(2,1)S(1)} %bitcast.8) | data formatting | bytes 1048576
